TPU v7x, 256 devices: a whole 4x4x8 slice. The times are simulated.
256 devices in a mesh: dp: 64 (over z, y, core), fsdp: 4 (over x).
Axes of the slice: x: 4, y: 4, z: 8, core: 2. Of those that a mesh axis runs over, the one named last changes fastest.
Arguments:
- feats: bfloat16 [64, 4, 8, 128, 256], P('dp', 'fsdp'), may hold values from -6 to 6
- grad_out: bfloat16 [64, 4, 8, 128, 256], P('dp', 'fsdp'), may hold values from -6 to 6
- kernel: bfloat16 [27, 256, 256], P(None, 'fsdp'), may hold values from -0.25 to 0.25
- send_bricks: int32 [64, 4, 64, 2], P('dp', 'fsdp'), may hold values from -1 to 7, as said below
- kmap: int32 [64, 4, 27, 2, 3], P('dp', 'fsdp'), may hold values from 0 to 135, as said below
- pair_count: int32 [64, 4, 27], P('dp', 'fsdp'), may hold values from 1 to 3, as said below
Outputs:
- out_feats: bfloat16 [64, 4, 8, 128, 256], P('dp', 'fsdp')
- in_grad: bfloat16 [64, 4, 8, 128, 256], P('dp', 'fsdp')
- kernel_grad: float32 [27, 256, 256], P(None, 'fsdp')
Inputs may be any that keep to these rules, and one draw needn't show every extreme that they name: `send_bricks`: entry (d, f, p, c) names the brick of device (d, f) sent to device (p, f) in slot c, or -1 for an empty slot. A device sends nothing to itself, fills exactly 48 slots, and fills both slots of at least one peer. kmap[d, f, t, 0, s] is an input brick of pool[d, f]: below 8 an own brick, else received slot p * 2 + c after the 8 own ones, and then always a slot that its sender filled. kmap[d, f, t, 1, s] is an output brick, below 8. Slots that are not live hold such ids too. `pair_count`: on some device every offset has 3 live slots.
All inputs are finite; a program needn't handle non-finite values.
Results may differ from a plain program's by a relative error of at most 0.0046.
Values may be sent and summed in bfloat16 or wider, within the bound.
No kernel may reach another device: no remote copies, remote signals or barrier semaphores. Data moves between devices by JAX's collectives and lax.ppermute only.
A program may use at most 192 MiB of HBM per device.

v0:
```python
import jax
import jax.numpy as jnp
from jax import lax
from jax.sharding import PartitionSpec as P


def on_device(feats, grad_out, kernel, send_bricks, kmap, pair_count):
    own_rows = feats[0, 0]
    upstream_rows = grad_out[0, 0]
    senders = send_bricks[0, 0]
    peer_total = senders.shape[0]
    slot_cap = senders.shape[1]
    brick_total = own_rows.shape[0]
    brick_rows = own_rows.shape[1]
    channels = own_rows.shape[2]
    filled = senders >= 0
    outgoing = own_rows[jnp.maximum(senders, 0)] * filled[:, :, None, None].astype(jnp.bfloat16)
    incoming = lax.all_to_all(outgoing, "dp", split_axis=0, concat_axis=0, tiled=True)
    weights = lax.all_gather(kernel, "fsdp", axis=1, tiled=True)
    pool = jnp.concatenate(
        [own_rows, incoming.reshape(peer_total * slot_cap, brick_rows, channels)], axis=0
    )
    pool_total = pool.shape[0]
    source_map = kmap[0, 0, :, 0, :]
    target_map = kmap[0, 0, :, 1, :]
    counts = pair_count[0, 0]
    tap_total = source_map.shape[0]
    slot_total = source_map.shape[1]
    active = (jnp.arange(slot_total)[None, :] < counts[:, None]).astype(jnp.bfloat16)
    inputs = pool[source_map] * active[:, :, None, None]
    upstream = upstream_rows[target_map] * active[:, :, None, None]
    contrib = jnp.einsum("tsvc,tcd->tsvd", inputs, weights, preferred_element_type=jnp.float32)
    produced = jax.ops.segment_sum(
        contrib.reshape(tap_total * slot_total, brick_rows, channels),
        target_map.reshape(-1),
        num_segments=brick_total,
    )
    backward = jnp.einsum("tsvd,tcd->tsvc", upstream, weights, preferred_element_type=jnp.float32)
    pool_grad = jax.ops.segment_sum(
        backward.reshape(tap_total * slot_total, brick_rows, channels),
        source_map.reshape(-1),
        num_segments=pool_total,
    )
    partial_value = jnp.einsum(
        "tsvc,tsvd->tcd", inputs, upstream, preferred_element_type=jnp.float32
    )
    ghosts = (
        pool_grad[brick_total:]
        .astype(jnp.bfloat16)
        .reshape(peer_total, slot_cap, brick_rows, channels)
    )
    returned = lax.all_to_all(ghosts, "dp", split_axis=0, concat_axis=0, tiled=True)
    owners = jnp.where(filled, senders, brick_total).reshape(-1)
    gathered_back = jax.ops.segment_sum(
        returned.reshape(peer_total * slot_cap, brick_rows, channels).astype(jnp.float32),
        owners,
        num_segments=brick_total + 1,
    )[:brick_total]
    in_grad = (pool_grad[:brick_total] + gathered_back).astype(jnp.bfloat16)
    divisor = jnp.float32(4 * lax.axis_size("dp") * lax.axis_size("fsdp"))
    shard_width = kernel.shape[1]
    summed = lax.psum(partial_value, ("dp", "fsdp"))
    portion = lax.dynamic_slice_in_dim(summed, lax.axis_index("fsdp") * shard_width, shard_width, 1)
    kernel_grad = portion / divisor
    return (produced.astype(jnp.bfloat16)[None, None], in_grad[None, None], kernel_grad)


def solution(mesh):
    placed = (
        P("dp", "fsdp", None, None, None),
        P("dp", "fsdp", None, None, None),
        P(None, "fsdp", None),
        P("dp", "fsdp", None, None),
        P("dp", "fsdp", None, None, None),
        P("dp", "fsdp", None),
    )
    return jax.shard_map(
        on_device,
        mesh=mesh,
        in_specs=placed,
        out_specs=(
            P("dp", "fsdp", None, None, None),
            P("dp", "fsdp", None, None, None),
            P(None, "fsdp", None),
        ),
        check_vma=False,
    )
```

profile of v0, /device:TPU:1, one launch (start us, length us, event | category | flops | bytes accessed | tf_op | source)
XLA Modules:
  0.0 671.1 jit_solution(8817993394391642369)
XLA Ops:
  8.0 0.7 fusion.20
  8.8 0.7 broadcast_maximum_fusion
  9.4 0.1 copy.22
  9.6 0.1 reshape.152
  9.8 7.5 %gather_fusion = bf16[128,128,256]{2,1,0:T(8,128)(2,1)} fusion(bf16[8,128,256]{2,1,0:T(8,128)(2,1)} %bitcast.48, s32[1024]{0:T(1024)S(1)} %pad_clamp_fusion.2), kind=kCustom, calls=%fused_computation | custom fusion | bytes 16777728 | tf_op jit(solution)/shard_map/gather | solution.py:17
  17.3 7.3 %broadcast_multiply_fusion = bf16[64,2,128,256]{3,2,1,0:T(8,128)(2,1)} fusion(bf16[64,2,128,256]{3,2,1,0:T(8,128)(2,1)} %bitcast.52, bf16[64,2]{1,0:T(8,128)(2,1)S(1)} %copy.22), kind=kLoop, calls=%fused_computation.16 | loop fusion | flops 4194304 | bytes 16777472 | tf_op jit(solution)/shard_map/mul | solution.py:17
  24.6 13.5 %all-to-all-start = ((bf16[64,2,128,256]{3,2,1,0:T(8,128)(2,1)}), bf16[64,2,128,256]{3,2,1,0:T(8,128)(2,1)}, u32[]{:S(2)}, u32[]{:S(2)}) async-start(bf16[64,2,128,256]{3,2,1,0:T(8,128)(2,1)} %broadcast_multiply_fusion), calls=%async_computation | async-start | bytes 16777216 | tf_op jit(solution)/shard_map/all_to_all | solution.py:18
  38.1 0.7 all-gather.2.cloned.1.call-update
  39.2 5.6 gather_fusion.2
  44.9 8.0 %copy.28 = bf16[27,3,128,256]{2,3,1,0:T(8,128)(2,1)} copy(bf16[27,3,128,256]{3,2,1,0:T(8,128)(2,1)} %bitcast.55) | data formatting | bytes 10616832 | tf_op jit(solution)/shard_map/gather | solution.py:31
  53.0 33.8 %all-gather.2.cloned.1.call-done = bf16[27,256,256]{2,1,0:T(8,128)(2,1)} async-done(((bf16[27,64,256]{2,1,0:T(8,128)(2,1)}), bf16[27,256,256]{2,1,0:T(8,128)(2,1)}) %all-gather.2.cloned.1.call-update) | async-done | bytes 3538960 | tf_op jit(solution)/shard_map/all_gather | solution.py:19
  86.7 9.4 %fusion.2 = f32[27,3,128,256]{3,2,1,0:T(8,128)} fusion(bf16[27,3,128,256]{2,3,1,0:T(8,128)(2,1)} %copy.28, bf16[27,256,256]{2,1,0:T(8,128)(2,1)} %all-gather.2.cloned.1.call-done, bf16[27,3]{1,0:T(8,128)(2,1)S(1)} %fusion.19), kind=kOutput, calls=%fused_computation.11 | convolution fusion | flops 1361608704 | bytes 19464354 | tf_op jit(solution)/shard_map/tsvd,tcd->tsvc/dot_general | solution.py:38
  96.1 8.4 %broadcast_in_dim.26 = f32[136,128,256]{2,1,0:T(8,128)} broadcast(f32[]{:T(128)} %constant.8.clone.1), dimensions={} | broadcast | bytes 17825796 | tf_op jit(solution)/shard_map/broadcast_in_dim | solution.py:39
  104.5 28.5 %scatter_fusion.1 = f32[136,128,256]{2,1,0:T(8,128)} fusion(f32[136,128,256]{2,1,0:T(8,128)} %broadcast_in_dim.26, s32[81]{0:T(128)S(1)} %reshape.184, f32[81,128,256]{2,1,0:T(8,128)} %bitcast.51), kind=kCustom, calls=%fused_computation.4 | custom fusion | flops 2654208 | bytes 31850820 | tf_op jit(solution)/shard_map/scatter-add | solution.py:39
  133.0 9.0 %slice.41 = bf16[128,128,256]{2,1,0:T(8,128)(2,1)} slice(f32[136,128,256]{2,1,0:T(8,128)} %scatter_fusion.1), slice={[8:136], [0:128], [0:256]} | slice | bytes 16777216 | tf_op jit(solution)/shard_map/slice | solution.py:48
  142.0 78.4 %all-to-all-done = bf16[64,2,128,256]{3,2,1,0:T(8,128)(2,1)} async-done(((bf16[64,2,128,256]{3,2,1,0:T(8,128)(2,1)}), bf16[64,2,128,256]{3,2,1,0:T(8,128)(2,1)}, u32[]{:S(2)}, u32[]{:S(2)}) %all-to-all-start) | async-done | bytes 8388640 | tf_op jit(solution)/shard_map/all_to_all | solution.py:18
  220.3 10.4 %all-to-all-start.1 = ((bf16[64,2,128,256]{3,2,1,0:T(8,128)(2,1)}), bf16[64,2,128,256]{3,2,1,0:T(8,128)(2,1)}, u32[]{:S(2)}, u32[]{:S(2)}) async-start(bf16[64,2,128,256]{3,2,1,0:T(8,128)(2,1)} %bitcast.53), calls=%async_computation.1 | async-start | bytes 16777216 | tf_op jit(solution)/shard_map/all_to_all | solution.py:52
  230.7 0.2 all-reduce.2.cloned.1.call-start
  231.2 7.6 %pad_maximum_fusion = bf16[136,128,256]{2,1,0:T(8,128)(2,1)} fusion(bf16[128,128,256]{2,1,0:T(8,128)(2,1)} %bitcast.3, bf16[8,128,256]{2,1,0:T(8,128)(2,1)S(1)} %bitcast.49), kind=kLoop, calls=%fused_computation.7 | loop fusion | flops 4456448 | bytes 17825792 | tf_op jit(solution)/shard_map/concatenate | solution.py:20
  238.8 9.2 %gather_fusion.1 = bf16[81,128,256]{2,1,0:T(8,128)(2,1)} fusion(bf16[136,128,256]{2,1,0:T(8,128)(2,1)} %pad_maximum_fusion, s32[1024]{0:T(1024)S(1)} %pad_clamp_fusion.1), kind=kCustom, calls=%fused_computation.1 | custom fusion | bytes 10617156 | tf_op jit(solution)/shard_map/gather | solution.py:30
  248.0 8.0 %copy.24 = bf16[27,3,128,256]{2,3,1,0:T(8,128)(2,1)} copy(bf16[27,3,128,256]{3,2,1,0:T(8,128)(2,1)} %bitcast.54) | data formatting | bytes 10616832 | tf_op jit(solution)/shard_map/gather | solution.py:30
  256.1 9.0 %fusion.9 = f32[27,256,256]{2,1,0:T(8,128)} fusion(bf16[27,3,128,256]{2,3,1,0:T(8,128)(2,1)} %copy.28, bf16[27,3,128,256]{2,3,1,0:T(8,128)(2,1)} %copy.24, bf16[27,3]{1,0:T(8,128)(2,1)S(1)} %fusion.19), kind=kOutput, calls=%fused_computation.19 | convolution fusion | flops 1364262912 | bytes 17694882 | tf_op jit(solution)/shard_map/tsvc,tsvd->tcd/dot_general | solution.py:44
  265.1 0.6 copy-done.4
  266.0 0.1 squeeze.19
  266.2 9.4 %fusion.5 = f32[27,3,128,256]{3,2,1,0:T(8,128)} fusion(bf16[27,3,128,256]{2,3,1,0:T(8,128)(2,1)} %copy.24, bf16[27,256,256]{2,1,0:T(8,128)(2,1)} %all-gather.2.cloned.1.call-done, bf16[27,3]{1,0:T(8,128)(2,1)S(1)} %fusion.19), kind=kOutput, calls=%fused_computation.14 | convolution fusion | flops 1361608704 | bytes 19464354 | tf_op jit(solution)/shard_map/tsvc,tcd->tsvd/dot_general | solution.py:32
  275.6 18.1 %scatter_fusion = f32[8,128,256]{2,1,0:T(8,128)S(1)} fusion(f32[8,128,256]{2,1,0:T(8,128)S(1)} %broadcast_in_dim.12, s32[81]{0:T(128)S(1)} %reshape.176, f32[81,128,256]{2,1,0:T(8,128)} %bitcast.50), kind=kCustom, calls=%fused_computation.3 | custom fusion | flops 2654208 | bytes 31850820 | tf_op jit(solution)/shard_map/scatter-add | solution.py:33
  293.7 0.8 convert_bitcast_fusion
  294.5 328.3 %all-reduce.2.cloned.1.call-done = f32[27,256,256]{2,1,0:T(8,128)} async-done(((f32[27,256,256]{2,1,0:T(8,128)}), f32[27,256,256]{2,1,0:T(8,128)}) %all-reduce.2.cloned.1.call-update) | async-done | bytes 7077904 | tf_op jit(solution)/shard_map/psum | solution.py:62
  622.8 2.9 dynamic-slice_multiply_fusion
  625.7 11.5 %bitcast_convert_fusion = f32[128,128,256]{2,1,0:T(8,128)} fusion(bf16[64,2,128,256]{3,2,1,0:T(8,128)(2,1)} %all-to-all-done.1), kind=kLoop, calls=%fused_computation.8 | loop fusion | flops 4194304 | bytes 25165824 | tf_op jit(solution)/shard_map/convert_element_type | solution.py:55
  637.3 24.2 %scatter_fusion.2 = f32[9,128,256]{2,1,0:T(8,128)S(1)} fusion(f32[9,128,256]{2,1,0:T(8,128)S(1)} %broadcast_in_dim.27, s32[128]{0:T(128)S(1)} %fusion.21, f32[128,128,256]{2,1,0:T(8,128)} %bitcast_convert_fusion), kind=kCustom, calls=%fused_computation.5 | custom fusion | flops 4194304 | bytes 50332160 | tf_op jit(solution)/shard_map/scatter-add | solution.py:54
  661.5 2.1 fusion.18
  (33 shorter events, 1.4 us)
Async XLA Ops:
  8.0 31.2 %copy-start = (bf16[1,1,8,128,256]{4,3,2,1,0:T(8,128)(2,1)S(1)}, bf16[1,1,8,128,256]{4,3,2,1,0:T(8,128)(2,1)}, u32[]{:S(2)}) copy-start(bf16[1,1,8,128,256]{4,3,2,1,0:T(8,128)(2,1)} %param.7) | copy-start | bytes 1572868
  24.6 14.2 %copy-start.3 = (s32[1,1,27,2,3]{2,3,4,1,0:T(2,128)S(1)}, s32[1,1,27,2,3]{2,3,4,1,0:T(2,128)}, u32[]{:S(2)}) copy-start(s32[1,1,27,2,3]{2,3,4,1,0:T(2,128)} %param.10) | copy-start | bytes 1948
  24.6 195.8 %all-to-all-start = ((bf16[64,2,128,256]{3,2,1,0:T(8,128)(2,1)}), bf16[64,2,128,256]{3,2,1,0:T(8,128)(2,1)}, u32[]{:S(2)}, u32[]{:S(2)}) async-start(bf16[64,2,128,256]{3,2,1,0:T(8,128)(2,1)} %broadcast_multiply_fusion), calls=%async_computation | async-start | bytes 16777216 | tf_op jit(solution)/shard_map/all_to_all | solution.py:18
  38.0 48.7 %all-gather.2.cloned.1.call-start = ((), (), s32[]{:S(2)}) async-start(), calls=%async_computation.2 | async-start | bytes 4423680 | tf_op jit(solution)/shard_map/all_gather | solution.py:19
  44.8 8.0 %copy-start.5 = (s32[1,1,27]{2,1,0:T(1,128)S(1)}, s32[1,1,27]{2,1,0:T(1,128)}, u32[]{:S(2)}) copy-start(s32[1,1,27]{2,1,0:T(1,128)} %param.11) | copy-start | bytes 328
  220.3 10.9 %copy-start.2 = (bf16[1,1,8,128,256]{4,3,2,1,0:T(8,128)(2,1)S(1)}, bf16[1,1,8,128,256]{4,3,2,1,0:T(8,128)(2,1)}, u32[]{:S(2)}) copy-start(bf16[1,1,8,128,256]{4,3,2,1,0:T(8,128)(2,1)} %param.6) | copy-start | bytes 1572868
  220.3 405.4 %all-to-all-start.1 = ((bf16[64,2,128,256]{3,2,1,0:T(8,128)(2,1)}), bf16[64,2,128,256]{3,2,1,0:T(8,128)(2,1)}, u32[]{:S(2)}, u32[]{:S(2)}) async-start(bf16[64,2,128,256]{3,2,1,0:T(8,128)(2,1)} %bitcast.53), calls=%async_computation.1 | async-start | bytes 16777216 | tf_op jit(solution)/shard_map/all_to_all | solution.py:52
  230.7 392.1 %all-reduce.2.cloned.1.call-start = ((), (), s32[]{:S(2)}) async-start(), calls=%async_computation.3 | async-start | bytes 14155776 | tf_op jit(solution)/shard_map/psum | solution.py:62
  265.1 0.7 copy-start.4
  637.3 26.3 %copy-start.1 = (bf16[1,1,8,128,256]{4,3,2,1,0:T(8,128)(2,1)S(1)}, bf16[1,1,8,128,256]{4,3,2,1,0:T(8,128)(2,1)}, u32[]{:S(2)}) copy-start(bf16[1,1,8,128,256]{4,3,2,1,0:T(8,128)(2,1)} %param.7) | copy-start | bytes 1572868
Sparse Core Ops, SparseCore 0:
  40.6 46.0 all-gather.1
Sparse Core Ops, SparseCore 1:
  265.2 357.6 all-reduce.1
where the time goes:
time: 673 us; the launch traced here: 671 us
  waiting for transfers between devices  441 us (66%)
  other arithmetic  105 us (16%)
  local copies, waits for them, and re-layouts  57.9 us (9%)
  matrix products  27.7 us (4%)
  starting transfers between devices  24.1 us (4%)
  between operations  15.6 us (2%)
    psum x1, waiting for transfers between devices, on_device(): summed = lax.psum(partial_value, ('dp', 'fsdp'))  328 us
    all_to_all x1, waiting for transfers between devices, on_device(): lax.all_to_all(outgoing, 'dp', split_axis=0, concat_axis=0, tiled=True)  78.4 us
    all_gather x1, waiting for transfers between devices, on_device(): weights = lax.all_gather(kernel, 'fsdp', axis=1, tiled=True)  33.8 us
    scatter-add x1, other arithmetic, on_device(): jax.ops.segment_sum(backward.reshape(tap_total * slot_total, brick_rows,...  28.5 us
    scatter-add x1, other arithmetic, on_device(): jax.ops.segment_sum(returned.reshape(peer_total * slot_cap, brick_rows, c...  24.2 us
    scatter-add x1, other arithmetic, on_device(): jax.ops.segment_sum(contrib.reshape(tap_total * slot_total, brick_rows, c...  18.1 us
    gather x2, local copies, waits for them, and re-layouts, on_device(): inputs = pool[source_map] * active[:, :, None, None]  17.2 us
    gather x2, local copies, waits for them, and re-layouts, on_device(): upstream = upstream_rows[target_map] * active[:, :, None, None]  13.7 us
  transfers between devices with their start and end apart: 4, of which 3 were waited for; matrix products, arithmetic and copies ran while one was open for 20% of the time, Pallas kernels for 0%

commit v1 on v0

v1 whole, which is shorter than its diff:
```python
import jax
import jax.numpy as jnp
from jax import lax
from jax.sharding import PartitionSpec as P


def _onehot(index, size, dtype):
    return (index[..., None] == jnp.arange(size, dtype=index.dtype)).astype(dtype)


def on_device(feats, grad_out, kernel, send_bricks, kmap, pair_count):
    own_rows = feats[0, 0]
    upstream_rows = grad_out[0, 0]
    senders = send_bricks[0, 0]
    peer_total, slot_cap = senders.shape
    brick_total, brick_rows, channels = own_rows.shape
    ghost_total = peer_total * slot_cap
    own_flat = own_rows.reshape(brick_total, brick_rows * channels)
    up_flat = upstream_rows.reshape(brick_total, brick_rows * channels)

    send_pick = _onehot(senders.reshape(-1), brick_total, jnp.bfloat16)
    outgoing = jnp.dot(send_pick, own_flat, preferred_element_type=jnp.float32).astype(jnp.bfloat16)
    outgoing = outgoing.reshape(peer_total, slot_cap, brick_rows, channels)
    incoming = lax.all_to_all(outgoing, "dp", split_axis=0, concat_axis=0, tiled=True)

    weights = lax.all_gather(kernel, "fsdp", axis=1, tiled=True)
    source_map = kmap[0, 0, :, 0, :]
    target_map = kmap[0, 0, :, 1, :]
    counts = pair_count[0, 0]
    tap_total, slot_total = source_map.shape
    pair_total = tap_total * slot_total
    active = jnp.arange(slot_total)[None, :] < counts[:, None]
    src = source_map.reshape(-1)
    tgt = target_map.reshape(-1)
    live = active.reshape(-1)

    up_pick = _onehot(tgt, brick_total, jnp.bfloat16) * live[:, None].astype(jnp.bfloat16)
    upstream = jnp.dot(up_pick, up_flat, preferred_element_type=jnp.float32).astype(jnp.bfloat16)
    upstream = upstream.reshape(tap_total, slot_total, brick_rows, channels)
    backward = jnp.einsum("tsvd,tcd->tsvc", upstream, weights, preferred_element_type=jnp.float32)
    backward = backward.reshape(pair_total, brick_rows * channels)
    src_pick = _onehot(src, brick_total + ghost_total, jnp.float32).T
    ghost_grad = jnp.dot(
        src_pick[brick_total:], backward, precision=lax.Precision.HIGHEST,
        preferred_element_type=jnp.float32,
    ).astype(jnp.bfloat16)
    own_grad = jnp.dot(
        src_pick[:brick_total], backward, precision=lax.Precision.HIGHEST,
        preferred_element_type=jnp.float32,
    )
    returned = lax.all_to_all(
        ghost_grad.reshape(peer_total, slot_cap, brick_rows, channels),
        "dp", split_axis=0, concat_axis=0, tiled=True,
    )

    in_pick = _onehot(src, brick_total + ghost_total, jnp.bfloat16) * live[:, None].astype(jnp.bfloat16)
    inc_flat = incoming.reshape(ghost_total, brick_rows * channels)
    inputs = (
        jnp.dot(in_pick[:, :brick_total], own_flat, preferred_element_type=jnp.float32)
        + jnp.dot(in_pick[:, brick_total:], inc_flat, preferred_element_type=jnp.float32)
    ).astype(jnp.bfloat16)
    inputs = inputs.reshape(tap_total, slot_total, brick_rows, channels)
    contrib = jnp.einsum("tsvc,tcd->tsvd", inputs, weights, preferred_element_type=jnp.float32)
    out_pick = _onehot(tgt, brick_total, jnp.float32).T
    produced = jnp.dot(
        out_pick, contrib.reshape(pair_total, brick_rows * channels),
        precision=lax.Precision.HIGHEST, preferred_element_type=jnp.float32,
    )
    produced = produced.reshape(brick_total, brick_rows, channels).astype(jnp.bfloat16)

    partial_value = jnp.einsum(
        "tsvc,tsvd->tcd", inputs, upstream, preferred_element_type=jnp.float32
    )
    divisor = jnp.float32(4 * lax.axis_size("dp") * lax.axis_size("fsdp"))
    scattered = lax.psum_scatter(partial_value, "fsdp", scatter_dimension=1, tiled=True)
    kernel_grad = lax.psum(scattered, "dp") / divisor

    owner_pick = _onehot(senders.reshape(-1), brick_total, jnp.bfloat16).T
    back_sum = jnp.dot(
        owner_pick, returned.reshape(ghost_total, brick_rows * channels),
        preferred_element_type=jnp.float32,
    )
    in_grad = (own_grad + back_sum).reshape(brick_total, brick_rows, channels).astype(jnp.bfloat16)
    return (produced[None, None], in_grad[None, None], kernel_grad)


def solution(mesh):
    placed = (
        P("dp", "fsdp", None, None, None),
        P("dp", "fsdp", None, None, None),
        P(None, "fsdp", None),
        P("dp", "fsdp", None, None),
        P("dp", "fsdp", None, None, None),
        P("dp", "fsdp", None),
    )
    return jax.shard_map(
        on_device,
        mesh=mesh,
        in_specs=placed,
        out_specs=(
            P("dp", "fsdp", None, None, None),
            P("dp", "fsdp", None, None, None),
            P(None, "fsdp", None),
        ),
        check_vma=False,
    )
```

time: 673 us -> 575 us (0.85)
  other arithmetic: 105 us -> 3.04 us
  waiting for transfers between devices: 441 us -> 368 us
  matrix products: 27.7 us -> 74.4 us
  local copies, waits for them, and re-layouts: 57.9 us -> 85.5 us
    psum x1, waiting for transfers between devices: 328 us -> 124 us  [on_device(): kernel_grad = lax.psum(scattered, 'dp') / divisor]
    unnamed x13 -> x33, local copies, waits for them, and re-layouts: 0.77 us -> 79.9 us
    scatter-add x3 -> x0, other arithmetic: 70.7 us -> none  [the longest x1 28.5 us: on_device(): jax.ops.segment_sum(backward.reshape(tap_total * slot_total, brick_rows,...]
    all_to_all x1, waiting for transfers between devices: 0.01 us -> 60.9 us  [on_device(): lax.all_to_all(ghost_grad.reshape(peer_total, slot_cap, brick_rows, chann...]
    dot_general x0 -> x8, matrix products: none -> 59.7 us  [the longest x1 13.3 us: on_device(): jnp.dot(out_pick, contrib.reshape(pair_total, brick_rows * channels), pre...]
    reduce_scatter x0 -> x1, waiting for transfers between devices: none -> 57 us  [on_device(): lax.psum_scatter(partial_value, 'fsdp', scatter_dimension=1, tiled=True)]
    gather x5 -> x0, local copies, waits for them, and re-layouts: 38.3 us -> none  [the longest x2 17.2 us: on_device(): inputs = pool[source_map] * active[:, :, None, None]]
    convert_element_type x3 -> x1, other arithmetic: 12.3 us -> 0.07 us  [on_device(): live[:, None].astype(jnp.bfloat16)]
  transfers between devices with their start and end apart: 4 -> 5, of which waited for: 3 -> 5; matrix products, arithmetic and copies ran while one was open for 20% -> 24% of each run, Pallas kernels for 0% -> 0%
where the time goes in v1:
time: 575 us; the launch traced here: 569 us
  waiting for transfers between devices  368 us (64%)
  local copies, waits for them, and re-layouts  85.5 us (15%)
  matrix products  74.4 us (13%)
  starting transfers between devices  24.6 us (4%)
  between operations  14.1 us (2%)
    psum x1, waiting for transfers between devices, on_device(): kernel_grad = lax.psum(scattered, 'dp') / divisor  124 us
    all_to_all x1, waiting for transfers between devices, on_device(): lax.all_to_all(outgoing, 'dp', split_axis=0, concat_axis=0, tiled=True)  84.7 us
    unnamed x33, local copies, waits for them, and re-layouts  79.9 us
    all_to_all x1, waiting for transfers between devices, on_device(): lax.all_to_all(ghost_grad.reshape(peer_total, slot_cap, brick_rows, chann...  60.9 us
    reduce_scatter x1, waiting for transfers between devices, on_device(): lax.psum_scatter(partial_value, 'fsdp', scatter_dimension=1, tiled=True)  57 us
    all_gather x1, waiting for transfers between devices, on_device(): weights = lax.all_gather(kernel, 'fsdp', axis=1, tiled=True)  41 us
    all_to_all x1, starting transfers between devices, on_device(): lax.all_to_all(outgoing, 'dp', split_axis=0, concat_axis=0, tiled=True)  13.5 us
    dot_general x1, matrix products, on_device(): jnp.dot(out_pick, contrib.reshape(pair_total, brick_rows * channels), pre...  13.3 us
  transfers between devices with their start and end apart: 5, of which 5 were waited for; matrix products, arithmetic and copies ran while one was open for 24% of the time, Pallas kernels for 0%

profile of v1, /device:TPU:1, one launch (start us, length us, event | category | flops | bytes accessed | tf_op | source)
XLA Modules:
  0.0 569.4 jit_solution(7112545395547521878)
XLA Ops:
  7.2 1.3 copy.25
  9.4 5.6 convolution_convert_fusion.1
  15.0 9.1 %copy.26 = bf16[16,8,128,256]{3,2,1,0:T(8,128)(2,1)} copy(bf16[16,8,128,256]{3,1,2,0:T(8,128)(2,1)} %bitcast.92) | data formatting | bytes 16777216
  24.2 13.5 %all-to-all-start = ((bf16[64,2,128,256]{3,2,1,0:T(8,128)(2,1)}), bf16[64,2,128,256]{3,2,1,0:T(8,128)(2,1)}, u32[]{:S(2)}, u32[]{:S(2)}) async-start(bf16[64,2,128,256]{3,2,1,0:T(8,128)(2,1)} %bitcast.90), calls=%async_computation | async-start | bytes 16777216 | tf_op jit(solution)/shard_map/all_to_all | solution.py:24
  39.3 1.7 convolution_convert_fusion.2
  41.0 1.5 copy.32
  42.5 2.7 slice.30
  45.3 41.0 %all-gather.2.cloned.1.call-done = bf16[27,256,256]{2,1,0:T(8,128)(2,1)} async-done(((bf16[27,64,256]{2,1,0:T(8,128)(2,1)}), bf16[27,256,256]{2,1,0:T(8,128)(2,1)}) %all-gather.2.cloned.1.call-update) | async-done | bytes 3538960 | tf_op jit(solution)/shard_map/all_gather | solution.py:26
  86.4 5.2 fusion.4
  91.5 6.0 %pad.1 = f32[88,128,256]{2,1,0:T(8,128)} pad(f32[81,128,256]{2,1,0:T(8,128)S(1)} %bitcast.87, f32[]{:T(128)} %constant.11), padding=0_7x0_0x0_0 | pad | bytes 22151172
  97.5 16.4 %copy.33 = f32[11,8,128,256]{3,1,2,0:T(8,128)} copy(f32[11,8,128,256]{3,2,1,0:T(8,128)} %bitcast.86) | data formatting | bytes 23068672
  113.9 12.2 %convolution_convert_fusion = bf16[128,32768]{1,0:T(8,128)(2,1)} fusion(f32[81,32768]{1,0:T(8,128)} %bitcast.77, pred[136,81]{1,0:T(8,128)(4,1)S(1)} %iota_compare_fusion.1), kind=kOutput, calls=%fused_computation | convolution fusion | flops 4081057792 | bytes 19021824 | tf_op jit(solution)/shard_map/dot_general | solution.py:43
  126.1 9.2 %copy.34 = bf16[16,8,128,256]{3,2,1,0:T(8,128)(2,1)} copy(bf16[16,8,128,256]{3,1,2,0:T(8,128)(2,1)} %bitcast.93) | data formatting | bytes 16777216
  135.3 84.7 %all-to-all-done = bf16[64,2,128,256]{3,2,1,0:T(8,128)(2,1)} async-done(((bf16[64,2,128,256]{3,2,1,0:T(8,128)(2,1)}), bf16[64,2,128,256]{3,2,1,0:T(8,128)(2,1)}, u32[]{:S(2)}, u32[]{:S(2)}) %all-to-all-start) | async-done | bytes 8388640 | tf_op jit(solution)/shard_map/all_to_all | solution.py:24
  219.9 10.3 %all-to-all-start.1 = ((bf16[64,2,128,256]{3,2,1,0:T(8,128)(2,1)}), bf16[64,2,128,256]{3,2,1,0:T(8,128)(2,1)}, u32[]{:S(2)}, u32[]{:S(2)}) async-start(bf16[64,2,128,256]{3,2,1,0:T(8,128)(2,1)} %bitcast.89), calls=%async_computation.1 | async-start | bytes 16777216 | tf_op jit(solution)/shard_map/all_to_all | solution.py:51
  230.5 5.9 %fusion.19 = f32[81,32768]{1,0:T(8,128)} fusion(bf16[8,32768]{1,0:T(8,128)(2,1)S(1)} %bitcast.99, bf16[81,136]{1,0:T(8,128)(2,1)S(1)} %fusion.14), kind=kOutput, calls=%fused_computation.26 | convolution fusion | flops 42467328 | bytes 11163648 | tf_op jit(solution)/shard_map/dot_general | solution.py:59
  236.3 12.4 %copy.27 = bf16[16,8,128,256]{3,1,2,0:T(8,128)(2,1)} copy(bf16[16,8,128,256]{3,2,1,0:T(8,128)(2,1)} %bitcast.20) | data formatting | bytes 16777216
  248.7 8.4 %fusion = bf16[81,32768]{1,0:T(8,128)(2,1)S(1)} fusion(f32[81,32768]{1,0:T(8,128)} %fusion.19, bf16[128,32768]{1,0:T(8,128)(2,1)} %bitcast.88, bf16[81,136]{1,0:T(8,128)(2,1)S(1)} %fusion.14), kind=kOutput, calls=%fused_computation.3 | convolution fusion | flops 684785664 | bytes 24336384 | tf_op jit(solution)/shard_map/dot_general | solution.py:60
  257.1 1.5 copy.28
  259.3 2.7 copy-done
  263.0 5.5 convolution_bitcast_fusion
  268.6 7.9 %fusion.25 = f32[8,32768]{1,0:T(8,128)} fusion(f32[81,32768]{1,0:T(8,128)} %bitcast.78, pred[136,81]{1,0:T(8,128)(4,1)} %copy-done.4), kind=kOutput, calls=%fused_computation.33 | convolution fusion | flops 254803968 | bytes 12583936 | tf_op jit(solution)/shard_map/dot_general | solution.py:47
  276.5 4.1 fusion.6
  280.6 4.9 slice_bitcast_fusion
  285.5 57.0 %reduce-scatter.2.cloned.1.call-done = f32[27,64,256]{2,1,0:T(8,128)} async-done(((f32[27,256,256]{2,1,0:T(8,128)}), f32[27,64,256]{2,1,0:T(8,128)}) %reduce-scatter.2.cloned.1.call-update) | async-done | bytes 1769488 | tf_op jit(solution)/shard_map/reduce_scatter | solution.py:75
  342.5 13.3 %fusion.11 = bf16[1,1,8,128,256]{4,2,3,1,0:T(8,128)(2,1)S(1)} fusion(f32[128,256,81]{1,0,2:T(8,128)} %slice_bitcast_fusion, s32[81]{0:T(128)S(1)} %eq.31), kind=kOutput, calls=%fused_computation.16 | convolution fusion | flops 255066752 | bytes 11141444 | tf_op jit(solution)/shard_map/dot_general | solution.py:65
  356.7 60.9 %all-to-all-done.1 = bf16[64,2,128,256]{3,2,1,0:T(8,128)(2,1)} async-done(((bf16[64,2,128,256]{3,2,1,0:T(8,128)(2,1)}), bf16[64,2,128,256]{3,2,1,0:T(8,128)(2,1)}, u32[]{:S(2)}, u32[]{:S(2)}) %all-to-all-start.1) | async-done | bytes 8388640 | tf_op jit(solution)/shard_map/all_to_all | solution.py:51
  417.6 12.5 %copy.35 = bf16[16,8,128,256]{3,1,2,0:T(8,128)(2,1)} copy(bf16[16,8,128,256]{3,2,1,0:T(8,128)(2,1)} %bitcast.50) | data formatting | bytes 16777216
  430.1 4.7 fusion.1
  434.8 0.9 copy.21
  435.7 124.1 %all-reduce.2.cloned.1.call-done = f32[27,64,256]{2,1,0:T(8,128)} async-done(((f32[27,64,256]{2,1,0:T(8,128)}), f32[27,64,256]{2,1,0:T(8,128)}) %all-reduce.2.cloned.1.call-update) | async-done | bytes 1769488 | tf_op jit(solution)/shard_map/psum | solution.py:76
  559.8 2.9 broadcast_multiply_fusion
  (38 shorter events, 5.6 us)
Async XLA Ops:
  24.2 14.2 %copy-start.5 = (s32[1,1,27,2,3]{2,3,4,1,0:T(2,128)S(1)}, s32[1,1,27,2,3]{2,3,4,1,0:T(2,128)}, u32[]{:S(2)}) copy-start(s32[1,1,27,2,3]{2,3,4,1,0:T(2,128)} %param.10) | copy-start | bytes 1948
  24.2 14.4 %copy-start.6 = (s32[1,1,27]{2,1,0:T(1,128)S(1)}, s32[1,1,27]{2,1,0:T(1,128)}, u32[]{:S(2)}) copy-start(s32[1,1,27]{2,1,0:T(1,128)} %param.11) | copy-start | bytes 328
  24.2 14.8 %copy-start.3 = (bf16[1,1,8,128,256]{4,3,2,1,0:T(8,128)(2,1)S(1)}, bf16[1,1,8,128,256]{4,3,2,1,0:T(8,128)(2,1)}, u32[]{:S(2)}) copy-start(bf16[1,1,8,128,256]{4,3,2,1,0:T(8,128)(2,1)} %param.7) | copy-start | bytes 1572868
  24.2 195.8 %all-to-all-start = ((bf16[64,2,128,256]{3,2,1,0:T(8,128)(2,1)}), bf16[64,2,128,256]{3,2,1,0:T(8,128)(2,1)}, u32[]{:S(2)}, u32[]{:S(2)}) async-start(bf16[64,2,128,256]{3,2,1,0:T(8,128)(2,1)} %bitcast.90), calls=%async_computation | async-start | bytes 16777216 | tf_op jit(solution)/shard_map/all_to_all | solution.py:24
  37.7 48.7 %all-gather.2.cloned.1.call-start = ((), (), s32[]{:S(2)}) async-start(), calls=%async_computation.3 | async-start | bytes 4423680 | tf_op jit(solution)/shard_map/all_gather | solution.py:26
  45.2 68.7 %copy-start.4 = (pred[136,81]{1,0:T(8,128)(4,1)}, pred[136,81]{1,0:T(8,128)(4,1)S(1)}, u32[]{:S(2)}) copy-start(pred[136,81]{1,0:T(8,128)(4,1)S(1)} %iota_compare_fusion.1) | copy-start | bytes 33052
  219.9 197.7 %all-to-all-start.1 = ((bf16[64,2,128,256]{3,2,1,0:T(8,128)(2,1)}), bf16[64,2,128,256]{3,2,1,0:T(8,128)(2,1)}, u32[]{:S(2)}, u32[]{:S(2)}) async-start(bf16[64,2,128,256]{3,2,1,0:T(8,128)(2,1)} %bitcast.89), calls=%async_computation.1 | async-start | bytes 16777216 | tf_op jit(solution)/shard_map/all_to_all | solution.py:51
  230.2 112.3 %reduce-scatter.2.cloned.1.call-start = ((), (), s32[]{:S(2)}) async-start(), calls=%async_computation.4 | async-start | bytes 8847360 | tf_op jit(solution)/shard_map/reduce_scatter | solution.py:75
  258.6 3.6 slice-start
  258.6 4.4 slice-start.1
  259.3 2.7 copy-start
  268.5 8.0 %copy-start.1 = (bf16[27,256,256]{2,1,0:T(8,128)(2,1)S(1)}, bf16[27,256,256]{2,1,0:T(8,128)(2,1)}, u32[]{:S(2)}) copy-start(bf16[27,256,256]{2,1,0:T(8,128)(2,1)} %all-gather.2.cloned.1.call-done) | copy-start | bytes 10616836
  268.5 291.3 %all-reduce.2.cloned.1.call-start = ((), (), s32[]{:S(2)}) async-start(), calls=%async_computation.5 | async-start | bytes 3538944 | tf_op jit(solution)/shard_map/psum | solution.py:76
  417.6 12.5 %copy-start.2 = (f32[8,32768]{1,0:T(8,128)S(1)}, f32[8,32768]{1,0:T(8,128)}, u32[]{:S(2)}) copy-start(f32[8,32768]{1,0:T(8,128)} %fusion.25) | copy-start | bytes 3145732
Sparse Core Ops, SparseCore 0:
  40.3 46.0 all-gather.1
  268.7 73.7 reduce-scatter.1
  345.9 213.8 all-reduce.1

commit v2 on v1

v2 whole, which is shorter than its diff:
```python
import jax
import jax.numpy as jnp
from jax import lax
from jax.sharding import PartitionSpec as P


def _onehot(index, size, dtype):
    return (index[..., None] == jnp.arange(size, dtype=index.dtype)).astype(dtype)


def _halving_doubling_sum(value, axis):
    size = lax.axis_size(axis)
    steps = size.bit_length() - 1
    assert 1 << steps == size
    me = lax.axis_index(axis)
    shape = value.shape
    buf = value.reshape(-1)
    total = buf.shape[0]
    assert total % size == 0
    for k in range(steps):
        half = buf.shape[0] // 2
        bit = (me >> k) & 1
        keep = lax.dynamic_slice_in_dim(buf, bit * half, half)
        send = lax.dynamic_slice_in_dim(buf, (1 - bit) * half, half)
        pairs = [(i, i ^ (1 << k)) for i in range(size)]
        buf = keep + lax.ppermute(send, axis, pairs)
    for k in reversed(range(steps)):
        part = buf.shape[0]
        bit = (me >> k) & 1
        pairs = [(i, i ^ (1 << k)) for i in range(size)]
        other = lax.ppermute(buf, axis, pairs)
        whole = jnp.zeros((2 * part,), buf.dtype)
        whole = lax.dynamic_update_slice_in_dim(whole, buf, bit * part, 0)
        buf = lax.dynamic_update_slice_in_dim(whole, other, (1 - bit) * part, 0)
    return buf.reshape(shape)


def on_device(feats, grad_out, kernel, send_bricks, kmap, pair_count):
    own_rows = feats[0, 0]
    upstream_rows = grad_out[0, 0]
    senders = send_bricks[0, 0]
    peer_total, slot_cap = senders.shape
    brick_total, brick_rows, channels = own_rows.shape
    ghost_total = peer_total * slot_cap

    send_pick = _onehot(senders.reshape(-1), brick_total, jnp.bfloat16)
    outgoing = jnp.einsum("pb,bvd->pvd", send_pick, own_rows, preferred_element_type=jnp.float32)
    outgoing = outgoing.astype(jnp.bfloat16).reshape(peer_total, slot_cap, brick_rows, channels)
    incoming = lax.all_to_all(outgoing, "dp", split_axis=0, concat_axis=0, tiled=True)

    weights = lax.all_gather(kernel, "fsdp", axis=1, tiled=True)
    source_map = kmap[0, 0, :, 0, :]
    target_map = kmap[0, 0, :, 1, :]
    counts = pair_count[0, 0]
    tap_total, slot_total = source_map.shape
    pair_total = tap_total * slot_total
    active = jnp.arange(slot_total)[None, :] < counts[:, None]
    src = source_map.reshape(-1)
    tgt = target_map.reshape(-1)
    live = active.reshape(-1)

    up_pick = _onehot(tgt, brick_total, jnp.bfloat16) * live[:, None].astype(jnp.bfloat16)
    upstream = jnp.einsum("pb,bvd->pvd", up_pick, upstream_rows, preferred_element_type=jnp.float32)
    upstream = upstream.astype(jnp.bfloat16)
    upstream = upstream.reshape(tap_total, slot_total, brick_rows, channels)
    backward = jnp.einsum("tsvd,tcd->tsvc", upstream, weights, preferred_element_type=jnp.float32)
    backward = backward.reshape(pair_total, brick_rows, channels)
    src_pick = _onehot(src, brick_total + ghost_total, jnp.float32).T
    ghost_grad = jnp.einsum(
        "ip,pvd->ivd", src_pick[brick_total:], backward, precision=lax.Precision.HIGHEST,
        preferred_element_type=jnp.float32,
    ).astype(jnp.bfloat16)
    own_grad = jnp.einsum(
        "ip,pvd->ivd", src_pick[:brick_total], backward, precision=lax.Precision.HIGHEST,
        preferred_element_type=jnp.float32,
    )
    returned = lax.all_to_all(
        ghost_grad.reshape(peer_total, slot_cap, brick_rows, channels),
        "dp", split_axis=0, concat_axis=0, tiled=True,
    )

    in_pick = _onehot(src, brick_total + ghost_total, jnp.bfloat16) * live[:, None].astype(jnp.bfloat16)
    inc_rows = incoming.reshape(ghost_total, brick_rows, channels)
    inputs = (
        jnp.einsum("pb,bvd->pvd", in_pick[:, :brick_total], own_rows, preferred_element_type=jnp.float32)
        + jnp.einsum("pb,bvd->pvd", in_pick[:, brick_total:], inc_rows, preferred_element_type=jnp.float32)
    ).astype(jnp.bfloat16)
    inputs = inputs.reshape(tap_total, slot_total, brick_rows, channels)
    contrib = jnp.einsum("tsvc,tcd->tsvd", inputs, weights, preferred_element_type=jnp.float32)
    out_pick = _onehot(tgt, brick_total, jnp.float32).T
    produced = jnp.einsum(
        "ip,pvd->ivd", out_pick, contrib.reshape(pair_total, brick_rows, channels),
        precision=lax.Precision.HIGHEST, preferred_element_type=jnp.float32,
    ).astype(jnp.bfloat16)

    partial_value = jnp.einsum(
        "tsvc,tsvd->tcd", inputs, upstream, preferred_element_type=jnp.float32
    )
    divisor = jnp.float32(4 * lax.axis_size("dp") * lax.axis_size("fsdp"))
    scattered = lax.psum_scatter(partial_value, "fsdp", scatter_dimension=1, tiled=True)
    kernel_grad = _halving_doubling_sum(scattered, "dp") / divisor

    owner_pick = _onehot(senders.reshape(-1), brick_total, jnp.bfloat16).T
    back_sum = jnp.einsum(
        "ip,pvd->ivd", owner_pick, returned.reshape(ghost_total, brick_rows, channels),
        preferred_element_type=jnp.float32,
    )
    in_grad = (own_grad + back_sum).astype(jnp.bfloat16)
    return (produced[None, None], in_grad[None, None], kernel_grad)


def solution(mesh):
    placed = (
        P("dp", "fsdp", None, None, None),
        P("dp", "fsdp", None, None, None),
        P(None, "fsdp", None),
        P("dp", "fsdp", None, None),
        P("dp", "fsdp", None, None, None),
        P("dp", "fsdp", None),
    )
    return jax.shard_map(
        on_device,
        mesh=mesh,
        in_specs=placed,
        out_specs=(
            P("dp", "fsdp", None, None, None),
            P("dp", "fsdp", None, None, None),
            P(None, "fsdp", None),
        ),
        check_vma=False,
    )
```

time: 575 us -> 643 us (1.12)
  local copies, waits for them, and re-layouts: 85.5 us -> 131 us
  starting transfers between devices: 24.6 us -> 46.9 us
    ppermute x0 -> x12, waiting for transfers between devices: none -> 180 us  [the longest x6 169 us: _halving_doubling_sum(): buf = keep + lax.ppermute(send, axis, pairs)]
    psum x1 -> x0, waiting for transfers between devices: 124 us -> none  [on_device(): kernel_grad = lax.psum(scattered, 'dp') / divisor]
    all_to_all x1, waiting for transfers between devices: 84.7 us -> 169 us  [on_device(): lax.all_to_all(outgoing, 'dp', split_axis=0, concat_axis=0, tiled=True)]
    reshape x0 -> x6, local copies, waits for them, and re-layouts: none -> 68.8 us  [the longest x2 21.3 us: on_device(): ghost_grad.reshape(peer_total, slot_cap, brick_rows, channels)]
    unnamed x33 -> x28, local copies, waits for them, and re-layouts: 79.9 us -> 11.4 us
    all_to_all x1, waiting for transfers between devices: 60.9 us -> 0.01 us  [on_device(): lax.all_to_all(ghost_grad.reshape(peer_total, slot_cap, brick_rows, chann...]
    all_gather x1, waiting for transfers between devices: 41 us -> 0.02 us  [on_device(): weights = lax.all_gather(kernel, 'fsdp', axis=1, tiled=True)]
    reduce_scatter x1, waiting for transfers between devices: 57 us -> 17 us  [on_device(): lax.psum_scatter(partial_value, 'fsdp', scatter_dimension=1, tiled=True)]
  transfers between devices with their start and end apart: 5 -> 16, of which waited for: 5 -> 12; matrix products, arithmetic and copies ran while one was open for 24% -> 26% of each run, Pallas kernels for 0% -> 0%
where the time goes in v2:
time: 643 us; the launch traced here: 638 us
  waiting for transfers between devices  367 us (57%)
  local copies, waits for them, and re-layouts  131 us (20%)
  matrix products  76.5 us (12%)
  starting transfers between devices  46.9 us (7%)
  between operations  14.7 us (2%)
    all_to_all x1, waiting for transfers between devices, on_device(): lax.all_to_all(outgoing, 'dp', split_axis=0, concat_axis=0, tiled=True)  169 us
    ppermute x6, waiting for transfers between devices, _halving_doubling_sum(): buf = keep + lax.ppermute(send, axis, pairs)  169 us
    reshape x2, local copies, waits for them, and re-layouts, on_device(): ghost_grad.reshape(peer_total, slot_cap, brick_rows, channels)  21.3 us
    reshape x2, local copies, waits for them, and re-layouts, on_device(): outgoing.astype(jnp.bfloat16)  21.2 us
    reduce_scatter x1, waiting for transfers between devices, on_device(): lax.psum_scatter(partial_value, 'fsdp', scatter_dimension=1, tiled=True)  17 us
    dot_general x1, matrix products, on_device(): jnp.einsum('ip,pvd->ivd', src_pick[brick_total:], backward, precision=lax...  15.4 us
    ppermute x6, starting transfers between devices, _halving_doubling_sum(): other = lax.ppermute(buf, axis, pairs)  15.1 us
    dynamic_update_slice x6, local copies, waits for them, and re-layouts, _halving_doubling_sum(): buf = lax.dynamic_update_slice_in_dim(whole, other, (1 - bit) * part, 0)  14.6 us
  transfers between devices with their start and end apart: 16, of which 12 were waited for; matrix products, arithmetic and copies ran while one was open for 26% of the time, Pallas kernels for 0%

profile of v2, /device:TPU:1, one launch (start us, length us, event | category | flops | bytes accessed | tf_op | source)
XLA Modules:
  0.0 637.7 jit_solution(12891325217901596341)
XLA Ops:
  8.2 5.6 convolution_convert_fusion
  13.9 13.1 %reshape.57 = bf16[64,2,128,256]{3,1,0,2:T(2,128)(2,1)} reshape(bf16[128,128,256]{2,0,1:T(8,128)(2,1)} %convolution_convert_fusion) | data formatting | bytes 16777216 | tf_op jit(solution)/shard_map/reshape | solution.py:48
  27.0 8.1 %copy.47 = bf16[64,2,128,256]{3,1,2,0:T(2,128)(2,1)} copy(bf16[64,2,128,256]{3,1,0,2:T(2,128)(2,1)} %reshape.57) | data formatting | bytes 16777216 | tf_op jit(solution)/shard_map/reshape | solution.py:48
  35.1 13.5 %all-to-all-start = ((bf16[64,2,128,256]{3,1,2,0:T(2,128)(2,1)}), bf16[64,2,128,256]{3,1,2,0:T(2,128)(2,1)}, u32[]{:S(2)}, u32[]{:S(2)}) async-start(bf16[64,2,128,256]{3,1,2,0:T(2,128)(2,1)} %copy.47), calls=%async_computation | async-start | bytes 16777216 | tf_op jit(solution)/shard_map/all_to_all | solution.py:49
  52.2 3.7 copy.53
  55.9 5.9 fusion.23
  61.8 169.1 %all-to-all-done = bf16[64,2,128,256]{3,1,2,0:T(2,128)(2,1)} async-done(((bf16[64,2,128,256]{3,1,2,0:T(2,128)(2,1)}), bf16[64,2,128,256]{3,1,2,0:T(2,128)(2,1)}, u32[]{:S(2)}, u32[]{:S(2)}) %all-to-all-start) | async-done | bytes 8388640 | tf_op jit(solution)/shard_map/all_to_all | solution.py:49
  230.9 8.1 %copy.48 = bf16[64,2,128,256]{3,1,0,2:T(2,128)(2,1)} copy(bf16[64,2,128,256]{3,1,2,0:T(2,128)(2,1)} %all-to-all-done) | data formatting | bytes 16777216 | tf_op jit(solution)/shard_map/all_to_all | solution.py:49
  239.0 13.2 %reshape.58 = bf16[128,128,256]{2,0,1:T(8,128)(2,1)} reshape(bf16[64,2,128,256]{3,1,0,2:T(2,128)(2,1)} %copy.48) | data formatting | bytes 16777216 | tf_op jit(solution)/shard_map/reshape | solution.py:83
  252.2 8.5 %add_convert_fusion = bf16[81,128,256]{2,0,1:T(8,128)(2,1)S(1)} fusion(f32[81,128,256]{2,0,1:T(8,128)} %fusion.23, bf16[128,128,256]{2,0,1:T(8,128)(2,1)} %reshape.58, bf16[81,136]{0,1:T(8,128)(2,1)S(1)} %fusion.25), kind=kOutput, calls=%fused_computation.2 | convolution fusion | flops 684785664 | bytes 24346624 | tf_op jit(solution)/shard_map/pb,bvd->pvd/dot_general | solution.py:86
  264.3 5.1 convolution_bitcast_fusion
  269.4 5.2 fusion.9
  274.6 3.9 copy-done.2
  278.6 15.4 %fusion.6 = bf16[128,128,256]{2,0,1:T(8,128)(2,1)} fusion(f32[81,128,256]{2,1,0:T(8,128)S(1)} %bitcast.69, pred[136,81]{1,0:T(8,128)(4,1)S(1)} %iota_compare_fusion), kind=kOutput, calls=%fused_computation.7 | convolution fusion | flops 4081057792 | bytes 19021824 | tf_op jit(solution)/shard_map/ip,pvd->ivd/dot_general | solution.py:69
  294.0 13.2 %reshape.63 = bf16[64,2,128,256]{3,1,0,2:T(2,128)(2,1)} reshape(bf16[128,128,256]{2,0,1:T(8,128)(2,1)} %fusion.6) | data formatting | bytes 16777216 | tf_op jit(solution)/shard_map/reshape | solution.py:78
  307.1 8.1 %copy.57 = bf16[64,2,128,256]{3,1,2,0:T(2,128)(2,1)} copy(bf16[64,2,128,256]{3,1,0,2:T(2,128)(2,1)} %reshape.63) | data formatting | bytes 16777216 | tf_op jit(solution)/shard_map/reshape | solution.py:78
  315.2 10.8 %all-to-all-start.1 = ((bf16[64,2,128,256]{3,1,2,0:T(2,128)(2,1)}), bf16[64,2,128,256]{3,1,2,0:T(2,128)(2,1)}, u32[]{:S(2)}, u32[]{:S(2)}) async-start(bf16[64,2,128,256]{3,1,2,0:T(2,128)(2,1)} %copy.57), calls=%async_computation.1 | async-start | bytes 16777216 | tf_op jit(solution)/shard_map/all_to_all | solution.py:77
  326.1 17.0 %reduce-scatter.2.cloned.1.call-done = f32[27,64,256]{2,1,0:T(8,128)} async-done(((f32[27,256,256]{2,1,0:T(8,128)}), f32[27,64,256]{2,1,0:T(8,128)}) %reduce-scatter.2.cloned.1.call-update) | async-done | bytes 1769488 | tf_op jit(solution)/shard_map/reduce_scatter | solution.py:100
  351.2 23.9 %collective-permute-done.1 = f32[110592]{0:T(1024)S(1)} collective-permute-done((f32[110592]{0:T(1024)S(1)}, f32[110592]{0:T(1024)S(1)}, u32[]{:S(2)}, u32[]{:S(2)}) %collective-permute-start.1) | collective-permute-done | bytes 442400 | tf_op jit(solution)/shard_map/ppermute | solution.py:26
  375.3 13.9 %collective-permute-done.2 = f32[55296]{0:T(1024)S(1)} collective-permute-done((f32[55296]{0:T(1024)S(1)}, f32[55296]{0:T(1024)S(1)}, u32[]{:S(2)}, u32[]{:S(2)}) %collective-permute-start.2) | collective-permute-done | bytes 221216 | tf_op jit(solution)/shard_map/ppermute | solution.py:26
  389.4 121.6 %collective-permute-done.3 = f32[27648]{0:T(1024)S(1)} collective-permute-done((f32[27648]{0:T(1024)S(1)}, f32[27648]{0:T(1024)S(1)}, u32[]{:S(2)}, u32[]{:S(2)}) %collective-permute-start.3) | collective-permute-done | bytes 110624 | tf_op jit(solution)/shard_map/ppermute | solution.py:26
  511.5 4.5 collective-permute-done.4
  516.2 4.3 collective-permute-start.5
  523.1 4.4 collective-permute-start.6
  542.5 13.2 %fusion.4 = f32[8,128,256]{2,0,1:T(8,128)S(1)} fusion(f32[81,128,256]{2,1,0:T(8,128)} %bitcast.70, pred[136,81]{1,0:T(8,128)(4,1)S(1)} %iota_compare_fusion), kind=kOutput, calls=%fused_computation.5 | convolution fusion | flops 254803968 | bytes 11666432 | tf_op jit(solution)/shard_map/ip,pvd->ivd/dot_general | solution.py:73
  569.5 7.2 %collective-permute-start.11 = (f32[221184]{0:T(1024)S(1)}, f32[221184]{0:T(1024)}, u32[]{:S(2)}, u32[]{:S(2)}) collective-permute-start(f32[221184]{0:T(1024)S(1)} %dynamic_update_slice.45), channel_id=1, source_target_pairs={{0,4},{4,0},{8,12},{12,8},{16,20},{20,16},{24,28},{28,24},{32,36},... | collective-permute-start | bytes 2654216 | tf_op jit(solution)/shard_map/ppermute | solution.py:31
  576.7 9.8 %fusion.17 = bf16[1,1,8,128,256]{4,2,3,1,0:T(8,128)(2,1)S(1)} fusion(f32[81,128,256]{2,1,0:T(8,128)S(1)} %bitcast.71, s32[81]{0:T(128)S(1)} %eq.31), kind=kOutput, calls=%fused_computation.18 | convolution fusion | flops 255066752 | bytes 11141444 | tf_op jit(solution)/shard_map/ip,pvd->ivd/dot_general | solution.py:91
  587.4 8.3 %copy.58 = bf16[64,2,128,256]{3,1,0,2:T(2,128)(2,1)} copy(bf16[64,2,128,256]{3,1,2,0:T(2,128)(2,1)} %all-to-all-done.1) | data formatting | bytes 16777216 | tf_op jit(solution)/shard_map/all_to_all | solution.py:77
  595.6 13.1 %reshape.64 = bf16[128,128,256]{2,0,1:T(8,128)(2,1)} reshape(bf16[64,2,128,256]{3,1,0,2:T(2,128)(2,1)} %copy.58) | data formatting | bytes 16777216 | tf_op jit(solution)/shard_map/reshape | solution.py:105
  608.8 4.6 fusion.20
  614.4 5.8 dynamic_update_slice.46
  620.2 8.6 %dynamic_update_slice.47 = f32[442368]{0:T(1024)S(1)} dynamic-update-slice(f32[442368]{0:T(1024)S(1)} %dynamic_update_slice.46, f32[221184]{0:T(1024)} %collective-permute-done.11, s32[]{:T(128)S(6)} %select_n.49) | dynamic-update-slice | bytes 1769476 | tf_op jit(solution)/shard_map/dynamic_update_slice | solution.py:34
  (94 shorter events, 52.3 us)
Async XLA Ops:
  7.2 1.1 copy-start
  35.1 14.8 %copy-start.6 = (s32[1,1,27,2,3]{2,3,4,1,0:T(2,128)S(1)}, s32[1,1,27,2,3]{2,3,4,1,0:T(2,128)}, u32[]{:S(2)}) copy-start(s32[1,1,27,2,3]{2,3,4,1,0:T(2,128)} %param.10) | copy-start | bytes 1948
  35.1 15.0 %copy-start.7 = (s32[1,1,27]{2,1,0:T(1,128)S(1)}, s32[1,1,27]{2,1,0:T(1,128)}, u32[]{:S(2)}) copy-start(s32[1,1,27]{2,1,0:T(1,128)} %param.11) | copy-start | bytes 328
  35.1 15.4 %copy-start.5 = (bf16[1,1,8,128,256]{4,3,2,1,0:T(8,128)(2,1)S(1)}, bf16[1,1,8,128,256]{4,3,2,1,0:T(8,128)(2,1)}, u32[]{:S(2)}) copy-start(bf16[1,1,8,128,256]{4,3,2,1,0:T(8,128)(2,1)} %param.7) | copy-start | bytes 1572868
  35.1 195.8 %all-to-all-start = ((bf16[64,2,128,256]{3,1,2,0:T(2,128)(2,1)}), bf16[64,2,128,256]{3,1,2,0:T(2,128)(2,1)}, u32[]{:S(2)}, u32[]{:S(2)}) async-start(bf16[64,2,128,256]{3,1,2,0:T(2,128)(2,1)} %copy.47), calls=%async_computation | async-start | bytes 16777216 | tf_op jit(solution)/shard_map/all_to_all | solution.py:49
  48.6 220.8 %all-gather.2.cloned.1.call-start = ((), (), s32[]{:S(2)}) async-start(), calls=%async_computation.3 | async-start | bytes 4423680 | tf_op jit(solution)/shard_map/all_gather | solution.py:51
  49.3 293.8 %reduce-scatter.2.cloned.1.call-start = ((), (), s32[]{:S(2)}) async-start(), calls=%async_computation.4 | async-start | bytes 8847360 | tf_op jit(solution)/shard_map/reduce_scatter | solution.py:100
  239.0 25.3 %slice-start.2 = ((s8[5308416]{0:T(1024)(128)(4,1)}), s8[1114112]{0:T(1024)(128)(4,1)S(1)}, s32[]{:S(2)}) async-start(s8[5308416]{0:T(1024)(128)(4,1)} %bitcast.77), calls=%async_computation.7 | async-start | bytes 2228224
  252.2 12.1 %slice-start.3 = ((s8[5308416]{0:T(1024)(128)(4,1)}), s8[4194304]{0:T(1024)(128)(4,1)S(1)}, s32[]{:S(2)}) async-start(s8[5308416]{0:T(1024)(128)(4,1)} %bitcast.77), calls=%async_computation.8 | async-start | bytes 8388608
  261.9 2.3 copy-start.3
  274.6 4.0 copy-start.2
  315.2 272.1 %all-to-all-start.1 = ((bf16[64,2,128,256]{3,1,2,0:T(2,128)(2,1)}), bf16[64,2,128,256]{3,1,2,0:T(2,128)(2,1)}, u32[]{:S(2)}, u32[]{:S(2)}) async-start(bf16[64,2,128,256]{3,1,2,0:T(2,128)(2,1)} %copy.57), calls=%async_computation.1 | async-start | bytes 16777216 | tf_op jit(solution)/shard_map/all_to_all | solution.py:77
  345.6 3.0 collective-permute-start
  349.9 25.2 %collective-permute-start.1 = (f32[110592]{0:T(1024)S(1)}, f32[110592]{0:T(1024)S(1)}, u32[]{:S(2)}, u32[]{:S(2)}) collective-permute-start(f32[110592]{0:T(1024)S(1)} %dynamic_slice.39), channel_id=1, source_target_pairs={{0,8},{4,12},{8,0},{12,4},{16,24},{20,28},{24,16},{28,20},{32,40},... | collective-permute-start | bytes 1327112 | tf_op jit(solution)/shard_map/ppermute | solution.py:26
  375.2 14.0 %collective-permute-start.2 = (f32[55296]{0:T(1024)S(1)}, f32[55296]{0:T(1024)S(1)}, u32[]{:S(2)}, u32[]{:S(2)}) collective-permute-start(f32[55296]{0:T(1024)S(1)} %dynamic_slice.41), channel_id=1, source_target_pairs={{0,16},{4,20},{8,24},{12,28},{16,0},{20,4},{24,8},{28,12},{32,48},... | collective-permute-start | bytes 663560 | tf_op jit(solution)/shard_map/ppermute | solution.py:26
  375.3 184.6 %slice-start = ((s8[5308416]{0:T(1024)(128)(4,1)}), s8[1114112]{0:T(1024)(128)(4,1)S(1)}, s32[]{:S(2)}) async-start(s8[5308416]{0:T(1024)(128)(4,1)} %bitcast.73), calls=%async_computation.5 | async-start | bytes 2228224
  389.3 121.7 %collective-permute-start.3 = (f32[27648]{0:T(1024)S(1)}, f32[27648]{0:T(1024)S(1)}, u32[]{:S(2)}, u32[]{:S(2)}) collective-permute-start(f32[27648]{0:T(1024)S(1)} %dynamic_slice.43), channel_id=1, source_target_pairs={{0,32},{4,36},{8,40},{12,44},{16,48},{20,52},{24,56},{28,60},{32,0... | collective-permute-start | bytes 331784 | tf_op jit(solution)/shard_map/ppermute | solution.py:26
  511.1 4.8 collective-permute-start.4
  516.2 6.7 %collective-permute-start.5 = (f32[6912]{0:T(1024)S(1)}, f32[6912]{0:T(1024)S(1)}, u32[]{:S(2)}, u32[]{:S(2)}) collective-permute-start(f32[6912]{0:T(1024)S(1)} %dynamic_slice.47), channel_id=1, source_target_pairs={{0,128},{4,132},{8,136},{12,140},{16,144},{20,148},{24,152},{28,15... | collective-permute-start | bytes 82952 | tf_op jit(solution)/shard_map/ppermute | solution.py:26
  523.1 6.7 %collective-permute-start.6 = (f32[6912]{0:T(1024)S(1)}, f32[6912]{0:T(1024)S(1)}, u32[]{:S(2)}, u32[]{:S(2)}) collective-permute-start(f32[6912]{0:T(1024)S(1)} %get-tuple-element.13), channel_id=1, source_target_pairs={{0,128},{4,132},{8,136},{12,140},{16,144},{20,148},{24,152},{28,15... | collective-permute-start | bytes 82952 | tf_op jit(solution)/shard_map/ppermute | solution.py:31
  530.2 4.3 collective-permute-start.7
  535.0 24.9 %copy-start.4 = (bf16[27,256,256]{2,1,0:T(8,128)(2,1)S(1)}, bf16[27,256,256]{2,1,0:T(8,128)(2,1)}, u32[]{:S(2)}) copy-start(bf16[27,256,256]{2,1,0:T(8,128)(2,1)} %all-gather.2.cloned.1.call-done) | copy-start | bytes 10616836
  535.0 4.3 collective-permute-start.8
  540.0 19.8 %slice-start.1 = ((s8[5308416]{0:T(1024)(128)(4,1)}), s8[4194304]{0:T(1024)(128)(4,1)S(1)}, s32[]{:S(2)}) async-start(s8[5308416]{0:T(1024)(128)(4,1)} %bitcast.73), calls=%async_computation.6 | async-start | bytes 8388608
  540.1 17.3 %collective-permute-start.9 = (f32[55296]{0:T(1024)S(1)}, f32[55296]{0:T(1024)S(1)}, u32[]{:S(2)}, u32[]{:S(2)}) collective-permute-start(f32[55296]{0:T(1024)S(1)} %dynamic_update_slice.41), channel_id=1, source_target_pairs={{0,16},{4,20},{8,24},{12,28},{16,0},{20,4},{24,8},{28,12},{32,48},... | collective-permute-start | bytes 663560 | tf_op jit(solution)/shard_map/ppermute | solution.py:31
  558.9 7.6 %collective-permute-start.10 = (f32[110592]{0:T(1024)S(1)}, f32[110592]{0:T(1024)S(1)}, u32[]{:S(2)}, u32[]{:S(2)}) collective-permute-start(f32[110592]{0:T(1024)S(1)} %dynamic_update_slice.43), channel_id=1, source_target_pairs={{0,8},{4,12},{8,0},{12,4},{16,24},{20,28},{24,16},{28,20},{32,40},... | collective-permute-start | bytes 1327112 | tf_op jit(solution)/shard_map/ppermute | solution.py:31
  569.5 50.8 %collective-permute-start.11 = (f32[221184]{0:T(1024)S(1)}, f32[221184]{0:T(1024)}, u32[]{:S(2)}, u32[]{:S(2)}) collective-permute-start(f32[221184]{0:T(1024)S(1)} %dynamic_update_slice.45), channel_id=1, source_target_pairs={{0,4},{4,0},{8,12},{12,8},{16,20},{20,16},{24,28},{28,24},{32,36},... | collective-permute-start | bytes 2654216 | tf_op jit(solution)/shard_map/ppermute | solution.py:31
  608.8 21.9 %copy-start.1 = (bf16[1,1,8,128,256]{4,3,2,1,0:T(8,128)(2,1)S(1)}, bf16[1,1,8,128,256]{4,3,2,1,0:T(8,128)(2,1)}, u32[]{:S(2)}) copy-start(bf16[1,1,8,128,256]{4,3,2,1,0:T(8,128)(2,1)} %param.6) | copy-start | bytes 1572868
Sparse Core Ops, SparseCore 0:
  51.2 46.0 all-gather.1
  269.5 73.5 reduce-scatter.1

commit v3 on v1

--- a/solution.py
+++ b/solution.py
@@ -6,6 +6,33 @@
 
 def _onehot(index, size, dtype):
     return (index[..., None] == jnp.arange(size, dtype=index.dtype)).astype(dtype)
+
+
+def _halving_doubling_sum(value, axis):
+    size = lax.axis_size(axis)
+    steps = size.bit_length() - 1
+    assert 1 << steps == size
+    me = lax.axis_index(axis)
+    shape = value.shape
+    buf = value.reshape(-1)
+    total = buf.shape[0]
+    assert total % size == 0
+    for k in range(steps):
+        half = buf.shape[0] // 2
+        bit = (me >> k) & 1
+        keep = lax.dynamic_slice_in_dim(buf, bit * half, half)
+        send = lax.dynamic_slice_in_dim(buf, (1 - bit) * half, half)
+        pairs = [(i, i ^ (1 << k)) for i in range(size)]
+        buf = keep + lax.ppermute(send, axis, pairs)
+    for k in reversed(range(steps)):
+        part = buf.shape[0]
+        bit = (me >> k) & 1
+        pairs = [(i, i ^ (1 << k)) for i in range(size)]
+        other = lax.ppermute(buf, axis, pairs)
+        whole = jnp.zeros((2 * part,), buf.dtype)
+        whole = lax.dynamic_update_slice_in_dim(whole, buf, bit * part, 0)
+        buf = lax.dynamic_update_slice_in_dim(whole, other, (1 - bit) * part, 0)
+    return buf.reshape(shape)
 
 
 def on_device(feats, grad_out, kernel, send_bricks, kmap, pair_count):
@@ -48,6 +75,7 @@
         src_pick[:brick_total], backward, precision=lax.Precision.HIGHEST,
         preferred_element_type=jnp.float32,
     )
+    incoming, ghost_grad = lax.optimization_barrier((incoming, ghost_grad))
     returned = lax.all_to_all(
         ghost_grad.reshape(peer_total, slot_cap, brick_rows, channels),
         "dp", split_axis=0, concat_axis=0, tiled=True,
@@ -73,7 +101,8 @@
     )
     divisor = jnp.float32(4 * lax.axis_size("dp") * lax.axis_size("fsdp"))
     scattered = lax.psum_scatter(partial_value, "fsdp", scatter_dimension=1, tiled=True)
-    kernel_grad = lax.psum(scattered, "dp") / divisor
+    scattered, returned = lax.optimization_barrier((scattered, returned))
+    kernel_grad = _halving_doubling_sum(scattered, "dp") / divisor
 
     owner_pick = _onehot(senders.reshape(-1), brick_total, jnp.bfloat16).T
     back_sum = jnp.dot(

time: 575 us -> 594 us (1.033)
  waiting for transfers between devices: 368 us -> 318 us
  local copies, waits for them, and re-layouts: 85.5 us -> 127 us
  starting transfers between devices: 24.6 us -> 50.2 us
    psum x1 -> x0, waiting for transfers between devices: 124 us -> none  [on_device(): kernel_grad = lax.psum(scattered, 'dp') / divisor]
    ppermute x0 -> x12, waiting for transfers between devices: none -> 38.7 us  [the longest x6 30.6 us: _halving_doubling_sum(): buf = keep + lax.ppermute(send, axis, pairs)]
    dynamic_update_slice x0 -> x11, local copies, waits for them, and re-layouts: none -> 29.4 us  [the longest x6 15.9 us: _halving_doubling_sum(): buf = lax.dynamic_update_slice_in_dim(whole, other, (1 - bit) * part, 0)]
    ppermute x0 -> x12, starting transfers between devices: none -> 25.9 us  [the longest x6 15.7 us: _halving_doubling_sum(): other = lax.ppermute(buf, axis, pairs)]
    reduce_scatter x1, waiting for transfers between devices: 57 us -> 74 us  [on_device(): lax.psum_scatter(partial_value, 'fsdp', scatter_dimension=1, tiled=True)]
    all_to_all x1, waiting for transfers between devices: 60.9 us -> 70.1 us  [on_device(): lax.all_to_all(ghost_grad.reshape(peer_total, slot_cap, brick_rows, chann...]
    all_to_all x1, waiting for transfers between devices: 84.7 us -> 93.7 us  [on_device(): lax.all_to_all(outgoing, 'dp', split_axis=0, concat_axis=0, tiled=True)]
    unnamed x33 -> x44, local copies, waits for them, and re-layouts: 79.9 us -> 85.8 us
  transfers between devices with their start and end apart: 5 -> 16, of which waited for: 5 -> 13; matrix products, arithmetic and copies ran while one was open for 24% -> 24% of each run, Pallas kernels for 0% -> 0%
where the time goes in v3:
time: 594 us; the launch traced here: 589 us
  waiting for transfers between devices  318 us (54%)
  local copies, waits for them, and re-layouts  127 us (21%)
  matrix products  74 us (12%)
  starting transfers between devices  50.2 us (8%)
  between operations  14.6 us (2%)
    all_to_all x1, waiting for transfers between devices, on_device(): lax.all_to_all(outgoing, 'dp', split_axis=0, concat_axis=0, tiled=True)  93.7 us
    unnamed x44, local copies, waits for them, and re-layouts  85.8 us
    reduce_scatter x1, waiting for transfers between devices, on_device(): lax.psum_scatter(partial_value, 'fsdp', scatter_dimension=1, tiled=True)  74 us
    all_to_all x1, waiting for transfers between devices, on_device(): lax.all_to_all(ghost_grad.reshape(peer_total, slot_cap, brick_rows, chann...  70.1 us
    all_gather x1, waiting for transfers between devices, on_device(): weights = lax.all_gather(kernel, 'fsdp', axis=1, tiled=True)  41.1 us
    ppermute x6, waiting for transfers between devices, _halving_doubling_sum(): buf = keep + lax.ppermute(send, axis, pairs)  30.6 us
    dynamic_update_slice x6, local copies, waits for them, and re-layouts, _halving_doubling_sum(): buf = lax.dynamic_update_slice_in_dim(whole, other, (1 - bit) * part, 0)  15.9 us
    ppermute x6, starting transfers between devices, _halving_doubling_sum(): other = lax.ppermute(buf, axis, pairs)  15.7 us
  transfers between devices with their start and end apart: 16, of which 13 were waited for; matrix products, arithmetic and copies ran while one was open for 24% of the time, Pallas kernels for 0%

profile of v3, /device:TPU:1, one launch (start us, length us, event | category | flops | bytes accessed | tf_op | source)
XLA Modules:
  0.0 588.5 jit_solution(1147493333370710091)
XLA Ops:
  9.4 5.7 convolution_convert_fusion.1
  15.1 9.2 %copy.26 = bf16[16,8,128,256]{3,2,1,0:T(8,128)(2,1)} copy(bf16[16,8,128,256]{3,1,2,0:T(8,128)(2,1)} %bitcast.95) | data formatting | bytes 16777216
  24.3 13.5 %all-to-all-start = ((bf16[64,2,128,256]{3,2,1,0:T(8,128)(2,1)}), bf16[64,2,128,256]{3,2,1,0:T(8,128)(2,1)}, u32[]{:S(2)}, u32[]{:S(2)}) async-start(bf16[64,2,128,256]{3,2,1,0:T(8,128)(2,1)} %bitcast.92), calls=%async_computation | async-start | bytes 16777216 | tf_op jit(solution)/shard_map/all_to_all | solution.py:51
  45.3 41.1 %all-gather.2.cloned.1.call-done = bf16[27,256,256]{2,1,0:T(8,128)(2,1)} async-done(((bf16[27,64,256]{2,1,0:T(8,128)(2,1)}), bf16[27,256,256]{2,1,0:T(8,128)(2,1)}) %all-gather.2.cloned.1.call-update) | async-done | bytes 3538960 | tf_op jit(solution)/shard_map/all_gather | solution.py:53
  86.4 5.2 fusion.6
  91.6 5.9 %pad = f32[88,128,256]{2,1,0:T(8,128)} pad(f32[81,128,256]{2,1,0:T(8,128)S(1)} %bitcast.89, f32[]{:T(128)} %constant.19.clone.1), padding=0_7x0_0x0_0 | pad | bytes 22151172
  97.5 16.7 %copy.29 = f32[11,8,128,256]{3,1,2,0:T(8,128)} copy(f32[11,8,128,256]{3,2,1,0:T(8,128)} %bitcast.88) | data formatting | bytes 23068672
  114.2 12.1 %convolution_convert_fusion = bf16[128,32768]{1,0:T(8,128)(2,1)} fusion(f32[81,32768]{1,0:T(8,128)} %bitcast.79, pred[136,81]{1,0:T(8,128)(4,1)S(1)} %iota_compare_fusion.1), kind=kOutput, calls=%fused_computation | convolution fusion | flops 4081057792 | bytes 19021824 | tf_op jit(solution)/shard_map/dot_general | solution.py:70
  126.4 93.7 %all-to-all-done = bf16[64,2,128,256]{3,2,1,0:T(8,128)(2,1)} async-done(((bf16[64,2,128,256]{3,2,1,0:T(8,128)(2,1)}), bf16[64,2,128,256]{3,2,1,0:T(8,128)(2,1)}, u32[]{:S(2)}, u32[]{:S(2)}) %all-to-all-start) | async-done | bytes 8388640 | tf_op jit(solution)/shard_map/all_to_all | solution.py:51
  220.0 9.2 %copy.34 = bf16[16,8,128,256]{3,2,1,0:T(8,128)(2,1)} copy(bf16[16,8,128,256]{3,1,2,0:T(8,128)(2,1)} %bitcast.93) | data formatting | bytes 16777216
  229.2 10.3 %all-to-all-start.1 = ((bf16[64,2,128,256]{3,2,1,0:T(8,128)(2,1)}), bf16[64,2,128,256]{3,2,1,0:T(8,128)(2,1)}, u32[]{:S(2)}, u32[]{:S(2)}) async-start(bf16[64,2,128,256]{3,2,1,0:T(8,128)(2,1)} %bitcast.91), calls=%async_computation.2 | async-start | bytes 16777216 | tf_op jit(solution)/shard_map/all_to_all | solution.py:79
  239.8 5.8 fusion.19
  245.6 12.3 %copy.30 = bf16[16,8,128,256]{3,1,2,0:T(8,128)(2,1)} copy(bf16[16,8,128,256]{3,2,1,0:T(8,128)(2,1)} %bitcast.31) | data formatting | bytes 16777216
  257.9 8.4 %fusion = bf16[81,32768]{1,0:T(8,128)(2,1)S(1)} fusion(f32[81,32768]{1,0:T(8,128)} %fusion.19, bf16[128,32768]{1,0:T(8,128)(2,1)} %bitcast.90, bf16[81,136]{1,0:T(8,128)(2,1)S(1)} %fusion.14), kind=kOutput, calls=%fused_computation.3 | convolution fusion | flops 684785664 | bytes 24336384 | tf_op jit(solution)/shard_map/dot_general | solution.py:88
  272.3 5.3 convolution_bitcast_fusion
  277.6 74.0 %reduce-scatter.2.cloned.1.call-done = f32[27,64,256]{2,1,0:T(8,128)} async-done(((f32[27,256,256]{2,1,0:T(8,128)}), f32[27,64,256]{2,1,0:T(8,128)}) %reduce-scatter.2.cloned.1.call-update) | async-done | bytes 1769488 | tf_op jit(solution)/shard_map/reduce_scatter | solution.py:103
  351.6 70.1 %all-to-all-done.1 = bf16[64,2,128,256]{3,2,1,0:T(8,128)(2,1)} async-done(((bf16[64,2,128,256]{3,2,1,0:T(8,128)(2,1)}), bf16[64,2,128,256]{3,2,1,0:T(8,128)(2,1)}, u32[]{:S(2)}, u32[]{:S(2)}) %all-to-all-start.1) | async-done | bytes 8388640 | tf_op jit(solution)/shard_map/all_to_all | solution.py:79
  424.2 4.5 collective-permute-start
  431.3 11.0 %collective-permute-done.1 = f32[110592]{0:T(1024)S(1)} collective-permute-done((f32[110592]{0:T(1024)S(1)}, f32[110592]{0:T(1024)S(1)}, u32[]{:S(2)}, u32[]{:S(2)}) %collective-permute-start.1) | collective-permute-done | bytes 442400 | tf_op jit(solution)/shard_map/ppermute | solution.py:26
  445.8 5.6 collective-permute-done.2
  467.4 6.3 %collective-permute-done.5 = f32[6912]{0:T(1024)} collective-permute-done((f32[6912]{0:T(1024)}, f32[6912]{0:T(1024)}, u32[]{:S(2)}, u32[]{:S(2)}) %collective-permute-start.5) | collective-permute-done | bytes 27680 | tf_op jit(solution)/shard_map/ppermute | solution.py:26
  476.5 6.0 %collective-permute-done.6 = f32[6912]{0:T(1024)S(1)} collective-permute-done((f32[6912]{0:T(1024)S(1)}, f32[6912]{0:T(1024)S(1)}, u32[]{:S(2)}, u32[]{:S(2)}) %collective-permute-start.6) | collective-permute-done | bytes 27680 | tf_op jit(solution)/shard_map/ppermute | solution.py:31
  497.8 7.8 %fusion.25 = f32[8,32768]{1,0:T(8,128)} fusion(f32[81,32768]{1,0:T(8,128)} %bitcast.80, pred[136,81]{1,0:T(8,128)(4,1)} %copy-done.8), kind=kOutput, calls=%fused_computation.39 | convolution fusion | flops 254803968 | bytes 12583936 | tf_op jit(solution)/shard_map/dot_general | solution.py:74
  509.4 4.1 fusion.4
  513.5 4.9 slice_bitcast_fusion
  521.4 4.6 dynamic_update_slice.45
  526.1 9.4 %collective-permute-start.11 = (f32[221184]{0:T(1024)S(1)}, f32[221184]{0:T(1024)S(1)}, u32[]{:S(2)}, u32[]{:S(2)}) collective-permute-start(f32[221184]{0:T(1024)S(1)} %dynamic_update_slice.45), channel_id=1, source_target_pairs={{0,4},{4,0},{8,12},{12,8},{16,20},{20,16},{24,28},{28,24},{32,36},... | collective-permute-start | bytes 2654216 | tf_op jit(solution)/shard_map/ppermute | solution.py:31
  535.5 13.3 %fusion.11 = bf16[1,1,8,128,256]{4,2,3,1,0:T(8,128)(2,1)S(1)} fusion(f32[128,256,81]{1,0,2:T(8,128)} %slice_bitcast_fusion, s32[81]{0:T(128)S(1)} %eq.31), kind=kOutput, calls=%fused_computation.16 | convolution fusion | flops 255066752 | bytes 11141444 | tf_op jit(solution)/shard_map/dot_general | solution.py:93
  549.7 12.5 %copy.35 = bf16[16,8,128,256]{3,1,2,0:T(8,128)(2,1)} copy(bf16[16,8,128,256]{3,2,1,0:T(8,128)(2,1)} %bitcast.50) | data formatting | bytes 16777216
  562.2 4.7 fusion.1
  567.9 5.8 dynamic_update_slice.46
  573.7 5.9 %dynamic_update_slice.47 = f32[442368]{0:T(1024)S(1)} dynamic-update-slice(f32[442368]{0:T(1024)S(1)} %dynamic_update_slice.46, f32[221184]{0:T(1024)S(1)} %collective-permute-done.11, s32[]{:T(128)S(6)} %select_n.49) | dynamic-update-slice | bytes 1769476 | tf_op jit(solution)/shard_map/dynamic_update_slice | solution.py:34
  (100 shorter events, 69.1 us)
Async XLA Ops:
  24.2 14.2 %copy-start.11 = (s32[1,1,27]{2,1,0:T(1,128)S(1)}, s32[1,1,27]{2,1,0:T(1,128)}, u32[]{:S(2)}) copy-start(s32[1,1,27]{2,1,0:T(1,128)} %param.11) | copy-start | bytes 328
  24.3 14.4 %copy-start.10 = (s32[1,1,27,2,3]{2,3,4,1,0:T(2,128)S(1)}, s32[1,1,27,2,3]{2,3,4,1,0:T(2,128)}, u32[]{:S(2)}) copy-start(s32[1,1,27,2,3]{2,3,4,1,0:T(2,128)} %param.10) | copy-start | bytes 1948
  24.3 14.8 %copy-start.5 = (bf16[1,1,8,128,256]{4,3,2,1,0:T(8,128)(2,1)S(1)}, bf16[1,1,8,128,256]{4,3,2,1,0:T(8,128)(2,1)}, u32[]{:S(2)}) copy-start(bf16[1,1,8,128,256]{4,3,2,1,0:T(8,128)(2,1)} %param.7) | copy-start | bytes 1572868
  24.3 195.8 %all-to-all-start = ((bf16[64,2,128,256]{3,2,1,0:T(8,128)(2,1)}), bf16[64,2,128,256]{3,2,1,0:T(8,128)(2,1)}, u32[]{:S(2)}, u32[]{:S(2)}) async-start(bf16[64,2,128,256]{3,2,1,0:T(8,128)(2,1)} %bitcast.92), calls=%async_computation | async-start | bytes 16777216 | tf_op jit(solution)/shard_map/all_to_all | solution.py:51
  37.7 48.7 %all-gather.2.cloned.1.call-start = ((), (), s32[]{:S(2)}) async-start(), calls=%async_computation.3 | async-start | bytes 4423680 | tf_op jit(solution)/shard_map/all_gather | solution.py:53
  45.3 69.0 %copy-start.8 = (pred[136,81]{1,0:T(8,128)(4,1)}, pred[136,81]{1,0:T(8,128)(4,1)S(1)}, u32[]{:S(2)}) copy-start(pred[136,81]{1,0:T(8,128)(4,1)S(1)} %iota_compare_fusion.1) | copy-start | bytes 33052
  229.2 192.6 %all-to-all-start.1 = ((bf16[64,2,128,256]{3,2,1,0:T(8,128)(2,1)}), bf16[64,2,128,256]{3,2,1,0:T(8,128)(2,1)}, u32[]{:S(2)}, u32[]{:S(2)}) async-start(bf16[64,2,128,256]{3,2,1,0:T(8,128)(2,1)} %bitcast.91), calls=%async_computation.2 | async-start | bytes 16777216 | tf_op jit(solution)/shard_map/all_to_all | solution.py:79
  239.5 112.1 %reduce-scatter.2.cloned.1.call-start = ((), (), s32[]{:S(2)}) async-start(), calls=%async_computation.4 | async-start | bytes 8847360 | tf_op jit(solution)/shard_map/reduce_scatter | solution.py:103
  267.8 3.6 slice-start
  267.9 4.4 slice-start.1
  268.5 2.7 copy-start
  424.2 6.5 %collective-permute-start = (f32[221184]{0:T(1024)S(1)}, f32[221184]{0:T(1024)S(1)}, u32[]{:S(2)}, u32[]{:S(2)}) collective-permute-start(f32[221184]{0:T(1024)S(1)} %dynamic_slice.37), channel_id=1, source_target_pairs={{0,4},{4,0},{8,12},{12,8},{16,20},{20,16},{24,28},{28,24},{32,36},... | collective-permute-start | bytes 2654216 | tf_op jit(solution)/shard_map/ppermute | solution.py:26
  430.9 11.4 %collective-permute-start.1 = (f32[110592]{0:T(1024)S(1)}, f32[110592]{0:T(1024)S(1)}, u32[]{:S(2)}, u32[]{:S(2)}) collective-permute-start(f32[110592]{0:T(1024)S(1)} %dynamic_slice.39), channel_id=1, source_target_pairs={{0,8},{4,12},{8,0},{12,4},{16,24},{20,28},{24,16},{28,20},{32,40},... | collective-permute-start | bytes 1327112 | tf_op jit(solution)/shard_map/ppermute | solution.py:26
  442.4 0.8 copy-start.3
  443.9 7.6 %collective-permute-start.2 = (f32[55296]{0:T(1024)}, f32[55296]{0:T(1024)}, u32[]{:S(2)}, u32[]{:S(2)}) collective-permute-start(f32[55296]{0:T(1024)} %dynamic_slice.41), channel_id=1, source_target_pairs={{0,16},{4,20},{8,24},{12,28},{16,0},{20,4},{24,8},{28,12},{32,48},... | collective-permute-start | bytes 663560 | tf_op jit(solution)/shard_map/ppermute | solution.py:26
  445.8 63.6 %copy-start.1 = (bf16[27,256,256]{2,1,0:T(8,128)(2,1)S(1)}, bf16[27,256,256]{2,1,0:T(8,128)(2,1)}, u32[]{:S(2)}) copy-start(bf16[27,256,256]{2,1,0:T(8,128)(2,1)} %all-gather.2.cloned.1.call-done) | copy-start | bytes 10616836
  452.5 0.7 copy-start.4
  453.9 3.9 collective-permute-start.3
  458.7 0.6 copy-start.6
  460.1 4.2 collective-permute-start.4
  465.3 0.6 copy-start.7
  466.6 7.1 %collective-permute-start.5 = (f32[6912]{0:T(1024)}, f32[6912]{0:T(1024)}, u32[]{:S(2)}, u32[]{:S(2)}) collective-permute-start(f32[6912]{0:T(1024)} %dynamic_slice.47), channel_id=1, source_target_pairs={{0,128},{4,132},{8,136},{12,140},{16,144},{20,148},{24,152},{28,15... | collective-permute-start | bytes 82952 | tf_op jit(solution)/shard_map/ppermute | solution.py:26
  475.8 6.6 %collective-permute-start.6 = (f32[6912]{0:T(1024)S(1)}, f32[6912]{0:T(1024)S(1)}, u32[]{:S(2)}, u32[]{:S(2)}) collective-permute-start(f32[6912]{0:T(1024)S(1)} %get-tuple-element.18), channel_id=1, source_target_pairs={{0,128},{4,132},{8,136},{12,140},{16,144},{20,148},{24,152},{28,15... | collective-permute-start | bytes 82952 | tf_op jit(solution)/shard_map/ppermute | solution.py:31
  482.5 0.6 copy-start.9
  484.6 4.4 collective-permute-start.7
  490.6 3.8 collective-permute-start.8
  495.2 12.1 %collective-permute-start.9 = (f32[55296]{0:T(1024)S(1)}, f32[55296]{0:T(1024)S(1)}, u32[]{:S(2)}, u32[]{:S(2)}) collective-permute-start(f32[55296]{0:T(1024)S(1)} %dynamic_update_slice.41), channel_id=1, source_target_pairs={{0,16},{4,20},{8,24},{12,28},{16,0},{20,4},{24,8},{28,12},{32,48},... | collective-permute-start | bytes 663560 | tf_op jit(solution)/shard_map/ppermute | solution.py:31
  508.8 12.6 %collective-permute-start.10 = (f32[110592]{0:T(1024)S(1)}, f32[110592]{0:T(1024)}, u32[]{:S(2)}, u32[]{:S(2)}) collective-permute-start(f32[110592]{0:T(1024)S(1)} %dynamic_update_slice.43), channel_id=1, source_target_pairs={{0,8},{4,12},{8,0},{12,4},{16,24},{20,28},{24,16},{28,20},{32,40},... | collective-permute-start | bytes 1327112 | tf_op jit(solution)/shard_map/ppermute | solution.py:31
  526.1 47.7 %collective-permute-start.11 = (f32[221184]{0:T(1024)S(1)}, f32[221184]{0:T(1024)S(1)}, u32[]{:S(2)}, u32[]{:S(2)}) collective-permute-start(f32[221184]{0:T(1024)S(1)} %dynamic_update_slice.45), channel_id=1, source_target_pairs={{0,4},{4,0},{8,12},{12,8},{16,20},{20,16},{24,28},{28,24},{32,36},... | collective-permute-start | bytes 2654216 | tf_op jit(solution)/shard_map/ppermute | solution.py:31
  549.7 12.5 %copy-start.2 = (f32[8,32768]{1,0:T(8,128)S(1)}, f32[8,32768]{1,0:T(8,128)}, u32[]{:S(2)}) copy-start(f32[8,32768]{1,0:T(8,128)} %fusion.25) | copy-start | bytes 3145732
Sparse Core Ops, SparseCore 0:
  40.3 46.0 all-gather.1
  277.7 73.8 reduce-scatter.1

commit v4 on v1

--- a/solution.py
+++ b/solution.py
@@ -6,6 +6,29 @@
 
 def _onehot(index, size, dtype):
     return (index[..., None] == jnp.arange(size, dtype=index.dtype)).astype(dtype)
+
+
+def _halve(buf, axis, k):
+    size = lax.axis_size(axis)
+    me = lax.axis_index(axis)
+    half = buf.shape[0] // 2
+    bit = (me >> k) & 1
+    keep = lax.dynamic_slice_in_dim(buf, bit * half, half)
+    send = lax.dynamic_slice_in_dim(buf, (1 - bit) * half, half)
+    pairs = [(i, i ^ (1 << k)) for i in range(size)]
+    return keep + lax.ppermute(send, axis, pairs)
+
+
+def _double(buf, axis, k):
+    size = lax.axis_size(axis)
+    me = lax.axis_index(axis)
+    part = buf.shape[0]
+    bit = (me >> k) & 1
+    pairs = [(i, i ^ (1 << k)) for i in range(size)]
+    other = lax.ppermute(buf, axis, pairs)
+    whole = jnp.zeros((2 * part,), buf.dtype)
+    whole = lax.dynamic_update_slice_in_dim(whole, buf, bit * part, 0)
+    return lax.dynamic_update_slice_in_dim(whole, other, (1 - bit) * part, 0)
 
 
 def on_device(feats, grad_out, kernel, send_bricks, kmap, pair_count):
@@ -48,6 +71,7 @@
         src_pick[:brick_total], backward, precision=lax.Precision.HIGHEST,
         preferred_element_type=jnp.float32,
     )
+    incoming, ghost_grad = lax.optimization_barrier((incoming, ghost_grad))
     returned = lax.all_to_all(
         ghost_grad.reshape(peer_total, slot_cap, brick_rows, channels),
         "dp", split_axis=0, concat_axis=0, tiled=True,
@@ -73,7 +97,19 @@
     )
     divisor = jnp.float32(4 * lax.axis_size("dp") * lax.axis_size("fsdp"))
     scattered = lax.psum_scatter(partial_value, "fsdp", scatter_dimension=1, tiled=True)
-    kernel_grad = lax.psum(scattered, "dp") / divisor
+    steps = lax.axis_size("dp").bit_length() - 1
+    assert 1 << steps == lax.axis_size("dp")
+    early = min(3, steps)
+    buf = scattered.reshape(-1)
+    assert buf.shape[0] % lax.axis_size("dp") == 0
+    for k in range(early):
+        buf = _halve(buf, "dp", k)
+    buf, returned, produced, own_grad = lax.optimization_barrier((buf, returned, produced, own_grad))
+    for k in range(early, steps):
+        buf = _halve(buf, "dp", k)
+    for k in reversed(range(steps)):
+        buf = _double(buf, "dp", k)
+    kernel_grad = buf.reshape(scattered.shape) / divisor
 
     owner_pick = _onehot(senders.reshape(-1), brick_total, jnp.bfloat16).T
     back_sum = jnp.dot(

time: 575 us -> 555 us (0.965)
  waiting for transfers between devices: 368 us -> 291 us
  local copies, waits for them, and re-layouts: 85.5 us -> 117 us
  starting transfers between devices: 24.6 us -> 49.2 us
    psum x1 -> x0, waiting for transfers between devices: 124 us -> none  [on_device(): kernel_grad = lax.psum(scattered, 'dp') / divisor]
    ppermute x0 -> x12, waiting for transfers between devices: none -> 32.6 us  [the longest x6 22 us: _halve(): return keep + lax.ppermute(send, axis, pairs)]
    ppermute x0 -> x12, starting transfers between devices: none -> 24.6 us  [the longest x6 13.9 us: _double(): other = lax.ppermute(buf, axis, pairs)]
    dynamic_update_slice x0 -> x11, local copies, waits for them, and re-layouts: none -> 24.1 us  [the longest x5 12 us: _double(): whole = lax.dynamic_update_slice_in_dim(whole, buf, bit * part, 0)]
    all_to_all x1, waiting for transfers between devices: 60.9 us -> 76 us  [on_device(): lax.all_to_all(ghost_grad.reshape(peer_total, slot_cap, brick_rows, chann...]
    all_to_all x1, waiting for transfers between devices: 84.7 us -> 93.5 us  [on_device(): lax.all_to_all(outgoing, 'dp', split_axis=0, concat_axis=0, tiled=True)]
    all_gather x1, waiting for transfers between devices: 41 us -> 34.9 us  [on_device(): weights = lax.all_gather(kernel, 'fsdp', axis=1, tiled=True)]
    unnamed x33 -> x42, local copies, waits for them, and re-layouts: 79.9 us -> 83.6 us
  transfers between devices with their start and end apart: 5 -> 16, of which waited for: 5 -> 11; matrix products, arithmetic and copies ran while one was open for 24% -> 24% of each run, Pallas kernels for 0% -> 0%
where the time goes in v4:
time: 555 us; the launch traced here: 550 us
  waiting for transfers between devices  291 us (52%)
  local copies, waits for them, and re-layouts  117 us (21%)
  matrix products  74.6 us (13%)
  starting transfers between devices  49.2 us (9%)
  between operations  14.9 us (3%)
    all_to_all x1, waiting for transfers between devices, on_device(): lax.all_to_all(outgoing, 'dp', split_axis=0, concat_axis=0, tiled=True)  93.5 us
    unnamed x42, local copies, waits for them, and re-layouts  83.6 us
    all_to_all x1, waiting for transfers between devices, on_device(): lax.all_to_all(ghost_grad.reshape(peer_total, slot_cap, brick_rows, chann...  76 us
    reduce_scatter x1, waiting for transfers between devices, on_device(): lax.psum_scatter(partial_value, 'fsdp', scatter_dimension=1, tiled=True)  53.5 us
    all_gather x1, waiting for transfers between devices, on_device(): weights = lax.all_gather(kernel, 'fsdp', axis=1, tiled=True)  34.9 us
    ppermute x6, waiting for transfers between devices, _halve(): return keep + lax.ppermute(send, axis, pairs)  22 us
    ppermute x6, starting transfers between devices, _double(): other = lax.ppermute(buf, axis, pairs)  13.9 us
    all_to_all x1, starting transfers between devices, on_device(): lax.all_to_all(outgoing, 'dp', split_axis=0, concat_axis=0, tiled=True)  13.5 us
  transfers between devices with their start and end apart: 16, of which 11 were waited for; matrix products, arithmetic and copies ran while one was open for 24% of the time, Pallas kernels for 0%

profile of v4, /device:TPU:1, one launch (start us, length us, event | category | flops | bytes accessed | tf_op | source)
XLA Modules:
  0.0 550.3 jit_solution(14746853181676875244)
XLA Ops:
  9.4 5.6 %convolution_convert_fusion.1 = bf16[128,32768]{1,0:T(8,128)(2,1)} fusion(bf16[8,32768]{1,0:T(8,128)(2,1)S(1)} %bitcast.101, s32[128]{0:T(128)S(1)} %eq.35), kind=kOutput, calls=%fused_computation.1 | convolution fusion | flops 71304192 | bytes 8913408 | tf_op jit(solution)/shard_map/dot_general | solution.py:45
  15.1 9.1 %copy.26 = bf16[16,8,128,256]{3,2,1,0:T(8,128)(2,1)} copy(bf16[16,8,128,256]{3,1,2,0:T(8,128)(2,1)} %bitcast.94) | data formatting | bytes 16777216
  24.2 13.5 %all-to-all-start = ((bf16[64,2,128,256]{3,2,1,0:T(8,128)(2,1)}), bf16[64,2,128,256]{3,2,1,0:T(8,128)(2,1)}, u32[]{:S(2)}, u32[]{:S(2)}) async-start(bf16[64,2,128,256]{3,2,1,0:T(8,128)(2,1)} %bitcast.91), calls=%async_computation | async-start | bytes 16777216 | tf_op jit(solution)/shard_map/all_to_all | solution.py:47
  45.6 5.8 %fusion.16 = f32[81,32768]{1,0:T(8,128)} fusion(bf16[8,32768]{1,0:T(8,128)(2,1)S(1)} %bitcast.102, bf16[81,136]{1,0:T(8,128)(2,1)S(1)} %fusion.10), kind=kOutput, calls=%fused_computation.31 | convolution fusion | flops 42467328 | bytes 11163648 | tf_op jit(solution)/shard_map/dot_general | solution.py:83
  51.4 34.9 %all-gather.2.cloned.1.call-done = bf16[27,256,256]{2,1,0:T(8,128)(2,1)} async-done(((bf16[27,64,256]{2,1,0:T(8,128)(2,1)}), bf16[27,256,256]{2,1,0:T(8,128)(2,1)}) %all-gather.2.cloned.1.call-update) | async-done | bytes 3538960 | tf_op jit(solution)/shard_map/all_gather | solution.py:49
  86.3 5.2 fusion.5
  91.5 5.9 %pad = f32[88,128,256]{2,1,0:T(8,128)} pad(f32[81,128,256]{2,1,0:T(8,128)S(1)} %bitcast.88, f32[]{:T(128)} %constant.11.clone.1), padding=0_7x0_0x0_0 | pad | bytes 22151172
  97.4 16.4 %copy.29 = f32[11,8,128,256]{3,1,2,0:T(8,128)} copy(f32[11,8,128,256]{3,2,1,0:T(8,128)} %bitcast.87) | data formatting | bytes 23068672
  113.8 12.6 %convolution_convert_fusion = bf16[128,32768]{1,0:T(8,128)(2,1)} fusion(f32[81,32768]{1,0:T(8,128)} %bitcast.78, pred[136,81]{1,0:T(8,128)(4,1)S(1)} %iota_compare_fusion.1), kind=kOutput, calls=%fused_computation | convolution fusion | flops 4081057792 | bytes 19021824 | tf_op jit(solution)/shard_map/dot_general | solution.py:66
  126.4 93.5 %all-to-all-done = bf16[64,2,128,256]{3,2,1,0:T(8,128)(2,1)} async-done(((bf16[64,2,128,256]{3,2,1,0:T(8,128)(2,1)}), bf16[64,2,128,256]{3,2,1,0:T(8,128)(2,1)}, u32[]{:S(2)}, u32[]{:S(2)}) %all-to-all-start) | async-done | bytes 8388640 | tf_op jit(solution)/shard_map/all_to_all | solution.py:47
  219.9 12.3 %copy.30 = bf16[16,8,128,256]{3,1,2,0:T(8,128)(2,1)} copy(bf16[16,8,128,256]{3,2,1,0:T(8,128)(2,1)} %bitcast.31) | data formatting | bytes 16777216
  232.3 8.5 %fusion = bf16[81,32768]{1,0:T(8,128)(2,1)S(1)} fusion(f32[81,32768]{1,0:T(8,128)} %fusion.16, bf16[128,32768]{1,0:T(8,128)(2,1)} %bitcast.89, bf16[81,136]{1,0:T(8,128)(2,1)S(1)} %fusion.10), kind=kOutput, calls=%fused_computation.3 | convolution fusion | flops 684785664 | bytes 24336384 | tf_op jit(solution)/shard_map/dot_general | solution.py:84
  246.7 5.1 convolution_bitcast_fusion
  251.8 9.3 %copy.33 = bf16[16,8,128,256]{3,2,1,0:T(8,128)(2,1)} copy(bf16[16,8,128,256]{3,1,2,0:T(8,128)(2,1)} %bitcast.92) | data formatting | bytes 16777216
  261.1 10.9 %all-to-all-start.1 = ((bf16[64,2,128,256]{3,2,1,0:T(8,128)(2,1)}), bf16[64,2,128,256]{3,2,1,0:T(8,128)(2,1)}, u32[]{:S(2)}, u32[]{:S(2)}) async-start(bf16[64,2,128,256]{3,2,1,0:T(8,128)(2,1)} %bitcast.90), calls=%async_computation.2 | async-start | bytes 16777216 | tf_op jit(solution)/shard_map/all_to_all | solution.py:75
  272.0 53.5 %reduce-scatter.2.cloned.1.call-done = f32[27,64,256]{2,1,0:T(8,128)} async-done(((f32[27,256,256]{2,1,0:T(8,128)}), f32[27,64,256]{2,1,0:T(8,128)}) %reduce-scatter.2.cloned.1.call-update) | async-done | bytes 1769488 | tf_op jit(solution)/shard_map/reduce_scatter | solution.py:99
  330.9 8.1 %fusion.22 = f32[8,32768]{1,0:T(8,128)} fusion(f32[81,32768]{1,0:T(8,128)} %bitcast.79, pred[136,81]{1,0:T(8,128)(4,1)} %copy-done.8), kind=kOutput, calls=%fused_computation.38 | convolution fusion | flops 254803968 | bytes 12583936 | tf_op jit(solution)/shard_map/dot_general | solution.py:70
  342.5 4.1 fusion.3
  346.6 4.9 slice_bitcast_fusion
  351.5 10.0 %collective-permute-done.1 = f32[110592]{0:T(1024)} collective-permute-done((f32[110592]{0:T(1024)}, f32[110592]{0:T(1024)}, u32[]{:S(2)}, u32[]{:S(2)}) %collective-permute-start.1) | collective-permute-done | bytes 442400 | tf_op jit(solution)/shard_map/ppermute | solution.py:19
  365.4 13.3 %fusion.7 = bf16[8,128,256]{2,0,1:T(8,128)(2,1)S(1)} fusion(f32[128,256,81]{1,0,2:T(8,128)} %slice_bitcast_fusion, s32[81]{0:T(128)S(1)} %eq.84), kind=kOutput, calls=%fused_computation.13 | convolution fusion | flops 255066752 | bytes 11141444 | tf_op jit(solution)/shard_map/dot_general | solution.py:89
  378.8 76.0 %all-to-all-done.1 = bf16[64,2,128,256]{3,2,1,0:T(8,128)(2,1)} async-done(((bf16[64,2,128,256]{3,2,1,0:T(8,128)(2,1)}), bf16[64,2,128,256]{3,2,1,0:T(8,128)(2,1)}, u32[]{:S(2)}, u32[]{:S(2)}) %all-to-all-start.1) | async-done | bytes 8388640 | tf_op jit(solution)/shard_map/all_to_all | solution.py:75
  454.7 4.5 collective-permute-start.3
  462.0 3.9 collective-permute-done.4
  467.5 5.5 collective-permute-done.5
  474.5 5.5 collective-permute-done.6
  489.5 3.4 collective-permute-start.9
  492.9 12.4 %copy.36 = bf16[16,8,128,256]{3,1,2,0:T(8,128)(2,1)} copy(bf16[16,8,128,256]{3,2,1,0:T(8,128)(2,1)} %bitcast.52) | data formatting | bytes 16777216
  508.7 4.7 fusion.11
  519.4 8.0 %collective-permute-start.11 = (f32[221184]{0:T(1024)S(1)}, f32[221184]{0:T(1024)S(1)}, u32[]{:S(2)}, u32[]{:S(2)}) collective-permute-start(f32[221184]{0:T(1024)S(1)} %dynamic_update_slice.45), channel_id=1, source_target_pairs={{0,4},{4,0},{8,12},{12,8},{16,20},{20,16},{24,28},{28,24},{32,36},... | collective-permute-start | bytes 2654216 | tf_op jit(solution)/shard_map/ppermute | solution.py:28
  529.4 5.8 %dynamic_update_slice.46 = f32[442368]{0:T(1024)S(1)} dynamic-update-slice(f32[442368]{0:T(1024)S(1)} %broadcast_in_dim.30, f32[221184]{0:T(1024)S(1)} %dynamic_update_slice.45, s32[]{:T(128)S(6)} %select_n.48) | dynamic-update-slice | bytes 1769476 | tf_op jit(solution)/shard_map/dynamic_update_slice | solution.py:30
  535.3 5.9 %dynamic_update_slice.47 = f32[442368]{0:T(1024)S(1)} dynamic-update-slice(f32[442368]{0:T(1024)S(1)} %dynamic_update_slice.46, f32[221184]{0:T(1024)S(1)} %collective-permute-done.11, s32[]{:T(128)S(6)} %select_n.49) | dynamic-update-slice | bytes 1769476 | tf_op jit(solution)/shard_map/dynamic_update_slice | solution.py:31
  (99 shorter events, 57.3 us)
Async XLA Ops:
  24.1 14.4 %copy-start.10 = (s32[1,1,27]{2,1,0:T(1,128)S(1)}, s32[1,1,27]{2,1,0:T(1,128)}, u32[]{:S(2)}) copy-start(s32[1,1,27]{2,1,0:T(1,128)} %param.11) | copy-start | bytes 328
  24.2 14.6 %copy-start.9 = (s32[1,1,27,2,3]{2,3,4,1,0:T(2,128)S(1)}, s32[1,1,27,2,3]{2,3,4,1,0:T(2,128)}, u32[]{:S(2)}) copy-start(s32[1,1,27,2,3]{2,3,4,1,0:T(2,128)} %param.10) | copy-start | bytes 1948
  24.2 15.1 %copy-start.7 = (bf16[1,1,8,128,256]{4,3,2,1,0:T(8,128)(2,1)S(1)}, bf16[1,1,8,128,256]{4,3,2,1,0:T(8,128)(2,1)}, u32[]{:S(2)}) copy-start(bf16[1,1,8,128,256]{4,3,2,1,0:T(8,128)(2,1)} %param.7) | copy-start | bytes 1572868
  24.2 195.8 %all-to-all-start = ((bf16[64,2,128,256]{3,2,1,0:T(8,128)(2,1)}), bf16[64,2,128,256]{3,2,1,0:T(8,128)(2,1)}, u32[]{:S(2)}, u32[]{:S(2)}) async-start(bf16[64,2,128,256]{3,2,1,0:T(8,128)(2,1)} %bitcast.91), calls=%async_computation | async-start | bytes 16777216 | tf_op jit(solution)/shard_map/all_to_all | solution.py:47
  37.6 48.7 %all-gather.2.cloned.1.call-start = ((), (), s32[]{:S(2)}) async-start(), calls=%async_computation.3 | async-start | bytes 4423680 | tf_op jit(solution)/shard_map/all_gather | solution.py:49
  38.4 287.2 %reduce-scatter.2.cloned.1.call-start = ((), (), s32[]{:S(2)}) async-start(), calls=%async_computation.4 | async-start | bytes 8847360 | tf_op jit(solution)/shard_map/reduce_scatter | solution.py:99
  45.5 68.3 %copy-start.8 = (pred[136,81]{1,0:T(8,128)(4,1)}, pred[136,81]{1,0:T(8,128)(4,1)S(1)}, u32[]{:S(2)}) copy-start(pred[136,81]{1,0:T(8,128)(4,1)S(1)} %iota_compare_fusion.1) | copy-start | bytes 33052
  242.3 3.6 slice-start
  242.3 4.4 slice-start.1
  243.0 2.7 copy-start
  261.1 193.6 %all-to-all-start.1 = ((bf16[64,2,128,256]{3,2,1,0:T(8,128)(2,1)}), bf16[64,2,128,256]{3,2,1,0:T(8,128)(2,1)}, u32[]{:S(2)}, u32[]{:S(2)}) async-start(bf16[64,2,128,256]{3,2,1,0:T(8,128)(2,1)} %bitcast.90), calls=%async_computation.2 | async-start | bytes 16777216 | tf_op jit(solution)/shard_map/all_to_all | solution.py:75
  327.9 1.2 copy-start.2
  330.1 12.4 %copy-start.1 = (bf16[27,256,256]{2,1,0:T(8,128)(2,1)S(1)}, bf16[27,256,256]{2,1,0:T(8,128)(2,1)}, u32[]{:S(2)}) copy-start(bf16[27,256,256]{2,1,0:T(8,128)(2,1)} %all-gather.2.cloned.1.call-done) | copy-start | bytes 10616836
  330.1 8.8 %collective-permute-start = (f32[221184]{0:T(1024)}, f32[221184]{0:T(1024)}, u32[]{:S(2)}, u32[]{:S(2)}) collective-permute-start(f32[221184]{0:T(1024)} %dynamic_slice.37), channel_id=1, source_target_pairs={{0,4},{4,0},{8,12},{12,8},{16,20},{20,16},{24,28},{28,24},{32,36},... | collective-permute-start | bytes 2654216 | tf_op jit(solution)/shard_map/ppermute | solution.py:19
  330.9 8.1 %copy-start.3 = (f32[216,2,8,128]{3,1,2,0:T(2,128)S(1)}, f32[216,2,8,128]{3,1,2,0:T(2,128)}, u32[]{:S(2)}) copy-start(f32[216,2,8,128]{3,1,2,0:T(2,128)} %copy-done.2) | copy-start | bytes 5308420
  340.2 1.1 copy-start.5
  341.3 20.2 %collective-permute-start.1 = (f32[110592]{0:T(1024)}, f32[110592]{0:T(1024)}, u32[]{:S(2)}, u32[]{:S(2)}) collective-permute-start(f32[110592]{0:T(1024)} %dynamic_slice.39), channel_id=1, source_target_pairs={{0,8},{4,12},{8,0},{12,4},{16,24},{20,28},{24,16},{28,20},{32,40},... | collective-permute-start | bytes 1327112 | tf_op jit(solution)/shard_map/ppermute | solution.py:19
  346.6 14.9 %copy-start.6 = (f32[221184]{0:T(1024)S(1)}, f32[221184]{0:T(1024)}, u32[]{:S(2)}) copy-start(f32[221184]{0:T(1024)} %copy-done.5) | copy-start | bytes 2654212
  362.6 16.1 %collective-permute-start.2 = (f32[55296]{0:T(1024)S(1)}, f32[55296]{0:T(1024)S(1)}, u32[]{:S(2)}, u32[]{:S(2)}) collective-permute-start(f32[55296]{0:T(1024)S(1)} %dynamic_slice.41), channel_id=1, source_target_pairs={{0,16},{4,20},{8,24},{12,28},{16,0},{20,4},{24,8},{28,12},{32,48},... | collective-permute-start | bytes 663560 | tf_op jit(solution)/shard_map/ppermute | solution.py:19
  454.7 7.0 %collective-permute-start.3 = (f32[27648]{0:T(1024)S(1)}, f32[27648]{0:T(1024)S(1)}, u32[]{:S(2)}, u32[]{:S(2)}) collective-permute-start(f32[27648]{0:T(1024)S(1)} %dynamic_slice.43), channel_id=1, source_target_pairs={{0,32},{4,36},{8,40},{12,44},{16,48},{20,52},{24,56},{28,60},{32,0... | collective-permute-start | bytes 331784 | tf_op jit(solution)/shard_map/ppermute | solution.py:19
  461.9 4.0 collective-permute-start.4
  466.1 6.9 %collective-permute-start.5 = (f32[6912]{0:T(1024)S(1)}, f32[6912]{0:T(1024)S(1)}, u32[]{:S(2)}, u32[]{:S(2)}) collective-permute-start(f32[6912]{0:T(1024)S(1)} %dynamic_slice.47), channel_id=1, source_target_pairs={{0,128},{4,132},{8,136},{12,140},{16,144},{20,148},{24,152},{28,15... | collective-permute-start | bytes 82952 | tf_op jit(solution)/shard_map/ppermute | solution.py:19
  473.2 6.7 %collective-permute-start.6 = (f32[6912]{0:T(1024)S(1)}, f32[6912]{0:T(1024)S(1)}, u32[]{:S(2)}, u32[]{:S(2)}) collective-permute-start(f32[6912]{0:T(1024)S(1)} %get-tuple-element.22), channel_id=1, source_target_pairs={{0,128},{4,132},{8,136},{12,140},{16,144},{20,148},{24,152},{28,15... | collective-permute-start | bytes 82952 | tf_op jit(solution)/shard_map/ppermute | solution.py:28
  480.4 4.2 collective-permute-start.7
  485.1 3.7 collective-permute-start.8
  489.5 17.5 %collective-permute-start.9 = (f32[55296]{0:T(1024)S(1)}, f32[55296]{0:T(1024)S(1)}, u32[]{:S(2)}, u32[]{:S(2)}) collective-permute-start(f32[55296]{0:T(1024)S(1)} %dynamic_update_slice.41), channel_id=1, source_target_pairs={{0,16},{4,20},{8,24},{12,28},{16,0},{20,4},{24,8},{28,12},{32,48},... | collective-permute-start | bytes 663560 | tf_op jit(solution)/shard_map/ppermute | solution.py:28
  505.3 22.1 %copy-start.4 = (f32[8,32768]{1,0:T(8,128)S(1)}, f32[8,32768]{1,0:T(8,128)}, u32[]{:S(2)}) copy-start(f32[8,32768]{1,0:T(8,128)} %fusion.22) | copy-start | bytes 3145732
  508.6 7.8 %collective-permute-start.10 = (f32[110592]{0:T(1024)S(1)}, f32[110592]{0:T(1024)S(1)}, u32[]{:S(2)}, u32[]{:S(2)}) collective-permute-start(f32[110592]{0:T(1024)S(1)} %dynamic_update_slice.43), channel_id=1, source_target_pairs={{0,8},{4,12},{8,0},{12,4},{16,24},{20,28},{24,16},{28,20},{32,40},... | collective-permute-start | bytes 1327112 | tf_op jit(solution)/shard_map/ppermute | solution.py:28
  519.4 15.9 %collective-permute-start.11 = (f32[221184]{0:T(1024)S(1)}, f32[221184]{0:T(1024)S(1)}, u32[]{:S(2)}, u32[]{:S(2)}) collective-permute-start(f32[221184]{0:T(1024)S(1)} %dynamic_update_slice.45), channel_id=1, source_target_pairs={{0,4},{4,0},{8,12},{12,8},{16,20},{20,16},{24,28},{28,24},{32,36},... | collective-permute-start | bytes 2654216 | tf_op jit(solution)/shard_map/ppermute | solution.py:28
Sparse Core Ops, SparseCore 0:
  40.3 46.0 all-gather.1
  251.9 73.5 reduce-scatter.1

commit v5 on v4

--- a/solution.py
+++ b/solution.py
@@ -22,16 +22,15 @@
 def _double(buf, axis, k):
     size = lax.axis_size(axis)
     me = lax.axis_index(axis)
-    part = buf.shape[0]
     bit = (me >> k) & 1
     pairs = [(i, i ^ (1 << k)) for i in range(size)]
     other = lax.ppermute(buf, axis, pairs)
-    whole = jnp.zeros((2 * part,), buf.dtype)
-    whole = lax.dynamic_update_slice_in_dim(whole, buf, bit * part, 0)
-    return lax.dynamic_update_slice_in_dim(whole, other, (1 - bit) * part, 0)
+    low_first = jnp.concatenate([buf, other])
+    high_first = jnp.concatenate([other, buf])
+    return jnp.where(bit == 0, low_first, high_first)
 
 
-def on_device(feats, grad_out, kernel, send_bricks, kmap, pair_count):
+def _section(feats, grad_out, kernel, send_bricks, kmap, pair_count):
     own_rows = feats[0, 0]
     upstream_rows = grad_out[0, 0]
     senders = send_bricks[0, 0]
@@ -71,7 +70,6 @@
         src_pick[:brick_total], backward, precision=lax.Precision.HIGHEST,
         preferred_element_type=jnp.float32,
     )
-    incoming, ghost_grad = lax.optimization_barrier((incoming, ghost_grad))
     returned = lax.all_to_all(
         ghost_grad.reshape(peer_total, slot_cap, brick_rows, channels),
         "dp", split_axis=0, concat_axis=0, tiled=True,
@@ -130,7 +128,7 @@
         P("dp", "fsdp", None),
     )
     return jax.shard_map(
-        on_device,
+        _section,
         mesh=mesh,
         in_specs=placed,
         out_specs=(

time: 555 us -> 576 us (1.038)
  waiting for transfers between devices: 291 us -> 337 us
  local copies, waits for them, and re-layouts: 117 us -> 94.2 us
    all_to_all x2, waiting for transfers between devices: 169 us -> 285 us  [the longest x1 168 us: _section(): lax.all_to_all(outgoing, 'dp', split_axis=0, concat_axis=0, tiled=True)]
    reduce_scatter x1, waiting for transfers between devices: 53.5 us -> 13.5 us  [_section(): lax.psum_scatter(partial_value, 'fsdp', scatter_dimension=1, tiled=True)]
    all_gather x1, waiting for transfers between devices: 34.9 us -> 0.02 us  [_section(): weights = lax.all_gather(kernel, 'fsdp', axis=1, tiled=True)]
    dynamic_update_slice x11 -> x0, local copies, waits for them, and re-layouts: 24.1 us -> none  [the longest x5 12 us: _double(): whole = lax.dynamic_update_slice_in_dim(whole, buf, bit * part, 0)]
  transfers between devices with their start and end apart: 16 -> 16, of which waited for: 11 -> 13; matrix products, arithmetic and copies ran while one was open for 24% -> 26% of each run, Pallas kernels for 0% -> 0%
where the time goes in v5:
time: 576 us; the launch traced here: 571 us
  waiting for transfers between devices  337 us (59%)
  local copies, waits for them, and re-layouts  94.2 us (16%)
  matrix products  74.2 us (13%)
  starting transfers between devices  47.3 us (8%)
  between operations  14.8 us (3%)
    all_to_all x1, waiting for transfers between devices, _section(): lax.all_to_all(outgoing, 'dp', split_axis=0, concat_axis=0, tiled=True)  168 us
    all_to_all x1, waiting for transfers between devices, _section(): lax.all_to_all(ghost_grad.reshape(peer_total, slot_cap, brick_rows, chann...  116 us
    unnamed x42, local copies, waits for them, and re-layouts  85 us
    ppermute x6, waiting for transfers between devices, _halve(): return keep + lax.ppermute(send, axis, pairs)  24.1 us
    ppermute x6, starting transfers between devices, _double(): other = lax.ppermute(buf, axis, pairs)  14.9 us
    ppermute x6, waiting for transfers between devices, _double(): other = lax.ppermute(buf, axis, pairs)  14.6 us
    reduce_scatter x1, waiting for transfers between devices, _section(): lax.psum_scatter(partial_value, 'fsdp', scatter_dimension=1, tiled=True)  13.5 us
    all_to_all x1, starting transfers between devices, _section(): lax.all_to_all(outgoing, 'dp', split_axis=0, concat_axis=0, tiled=True)  13.5 us
  transfers between devices with their start and end apart: 16, of which 13 were waited for; matrix products, arithmetic and copies ran while one was open for 26% of the time, Pallas kernels for 0%

profile of v5, /device:TPU:1, one launch (start us, length us, event | category | flops | bytes accessed | tf_op | source)
XLA Modules:
  0.0 571.1 jit_solution(2993309118843000837)
XLA Ops:
  9.4 5.6 convolution_convert_fusion.1
  15.1 9.2 %copy.26 = bf16[16,8,128,256]{3,2,1,0:T(8,128)(2,1)} copy(bf16[16,8,128,256]{3,1,2,0:T(8,128)(2,1)} %bitcast.93) | data formatting | bytes 16777216
  24.2 13.5 %all-to-all-start = ((bf16[64,2,128,256]{3,2,1,0:T(8,128)(2,1)}), bf16[64,2,128,256]{3,2,1,0:T(8,128)(2,1)}, u32[]{:S(2)}, u32[]{:S(2)}) async-start(bf16[64,2,128,256]{3,2,1,0:T(8,128)(2,1)} %bitcast.91), calls=%async_computation | async-start | bytes 16777216 | tf_op jit(solution)/shard_map/all_to_all | solution.py:46
  42.9 2.8 slice.29
  45.7 5.8 %fusion.17 = f32[81,32768]{1,0:T(8,128)} fusion(bf16[8,32768]{1,0:T(8,128)(2,1)S(1)} %bitcast.102, bf16[81,136]{1,0:T(8,128)(2,1)S(1)} %fusion.11), kind=kOutput, calls=%fused_computation.37 | convolution fusion | flops 42467328 | bytes 11163648 | tf_op jit(solution)/shard_map/dot_general | solution.py:81
  51.5 168.5 %all-to-all-done = bf16[64,2,128,256]{3,2,1,0:T(8,128)(2,1)} async-done(((bf16[64,2,128,256]{3,2,1,0:T(8,128)(2,1)}), bf16[64,2,128,256]{3,2,1,0:T(8,128)(2,1)}, u32[]{:S(2)}, u32[]{:S(2)}) %all-to-all-start) | async-done | bytes 8388640 | tf_op jit(solution)/shard_map/all_to_all | solution.py:46
  220.0 12.4 %copy.27 = bf16[16,8,128,256]{3,1,2,0:T(8,128)(2,1)} copy(bf16[16,8,128,256]{3,2,1,0:T(8,128)(2,1)} %bitcast.19) | data formatting | bytes 16777216
  232.4 8.8 %fusion = bf16[81,32768]{1,0:T(8,128)(2,1)S(1)} fusion(f32[81,32768]{1,0:T(8,128)} %fusion.17, bf16[128,32768]{1,0:T(8,128)(2,1)} %bitcast.89, bf16[81,136]{1,0:T(8,128)(2,1)S(1)} %fusion.11), kind=kOutput, calls=%fused_computation.3 | convolution fusion | flops 684785664 | bytes 24336384 | tf_op jit(solution)/shard_map/dot_general | solution.py:82
  243.5 2.7 copy-done
  247.2 5.0 convolution_bitcast_fusion
  252.3 5.2 fusion.5
  257.4 5.9 %pad.24 = f32[88,128,256]{2,1,0:T(8,128)} pad(f32[81,128,256]{2,1,0:T(8,128)S(1)} %bitcast.88, f32[]{:T(128)} %constant.55), padding=0_7x0_0x0_0 | pad | bytes 22151172
  263.3 17.7 %copy.32 = f32[11,8,128,256]{3,1,2,0:T(8,128)} copy(f32[11,8,128,256]{3,2,1,0:T(8,128)} %bitcast.87) | data formatting | bytes 23068672
  281.0 12.2 %convolution_convert_fusion = bf16[128,32768]{1,0:T(8,128)(2,1)} fusion(f32[81,32768]{1,0:T(8,128)} %bitcast.78, pred[136,81]{1,0:T(8,128)(4,1)S(1)} %iota_compare_fusion.1), kind=kOutput, calls=%fused_computation | convolution fusion | flops 4081057792 | bytes 19021824 | tf_op jit(solution)/shard_map/dot_general | solution.py:65
  293.2 9.2 %copy.33 = bf16[16,8,128,256]{3,2,1,0:T(8,128)(2,1)} copy(bf16[16,8,128,256]{3,1,2,0:T(8,128)(2,1)} %bitcast.94) | data formatting | bytes 16777216
  302.4 10.0 %all-to-all-start.1 = ((bf16[64,2,128,256]{3,2,1,0:T(8,128)(2,1)}), bf16[64,2,128,256]{3,2,1,0:T(8,128)(2,1)}, u32[]{:S(2)}, u32[]{:S(2)}) async-start(bf16[64,2,128,256]{3,2,1,0:T(8,128)(2,1)} %bitcast.90), calls=%async_computation.2 | async-start | bytes 16777216 | tf_op jit(solution)/shard_map/all_to_all | solution.py:73
  312.4 13.5 %reduce-scatter.2.cloned.1.call-done = f32[27,64,256]{2,1,0:T(8,128)} async-done(((f32[27,256,256]{2,1,0:T(8,128)}), f32[27,64,256]{2,1,0:T(8,128)}) %reduce-scatter.2.cloned.1.call-update) | async-done | bytes 1769488 | tf_op jit(solution)/shard_map/reduce_scatter | solution.py:97
  331.5 7.9 %fusion.23 = f32[8,32768]{1,0:T(8,128)} fusion(f32[81,32768]{1,0:T(8,128)} %bitcast.79, pred[136,81]{1,0:T(8,128)(4,1)} %copy-done.8), kind=kOutput, calls=%fused_computation.44 | convolution fusion | flops 254803968 | bytes 12583936 | tf_op jit(solution)/shard_map/dot_general | solution.py:69
  342.9 4.1 fusion.3
  347.0 4.8 slice_bitcast_fusion
  351.8 10.4 %collective-permute-done.1 = f32[110592]{0:T(1024)} collective-permute-done((f32[110592]{0:T(1024)}, f32[110592]{0:T(1024)}, u32[]{:S(2)}, u32[]{:S(2)}) %collective-permute-start.1) | collective-permute-done | bytes 442400 | tf_op jit(solution)/shard_map/ppermute | solution.py:19
  363.4 13.2 %fusion.8 = bf16[8,128,256]{2,0,1:T(8,128)(2,1)S(1)} fusion(f32[128,256,81]{1,0,2:T(8,128)} %slice_bitcast_fusion, s32[81]{0:T(128)S(1)} %eq.99), kind=kOutput, calls=%fused_computation.15 | convolution fusion | flops 255066752 | bytes 11141444 | tf_op jit(solution)/shard_map/dot_general | solution.py:87
  378.6 116.1 %all-to-all-done.1 = bf16[64,2,128,256]{3,2,1,0:T(8,128)(2,1)} async-done(((bf16[64,2,128,256]{3,2,1,0:T(8,128)(2,1)}), bf16[64,2,128,256]{3,2,1,0:T(8,128)(2,1)}, u32[]{:S(2)}, u32[]{:S(2)}) %all-to-all-start.1) | async-done | bytes 8388640 | tf_op jit(solution)/shard_map/all_to_all | solution.py:73
  494.7 4.9 collective-permute-start.3
  502.0 3.9 collective-permute-done.4
  507.6 5.6 collective-permute-done.5
  514.3 5.7 collective-permute-done.6
  520.1 4.2 collective-permute-done.7
  528.4 3.0 collective-permute-start.9
  531.4 12.4 %copy.36 = bf16[16,8,128,256]{3,1,2,0:T(8,128)(2,1)} copy(bf16[16,8,128,256]{3,2,1,0:T(8,128)(2,1)} %bitcast.52) | data formatting | bytes 16777216
  543.9 4.8 fusion.12
  551.2 8.7 %collective-permute-start.11 = (f32[221184]{0:T(1024)S(1)}, f32[221184]{0:T(1024)S(1)}, u32[]{:S(2)}, u32[]{:S(2)}) collective-permute-start(f32[221184]{0:T(1024)S(1)} %maximum_select_fusion.1), channel_id=1, source_target_pairs={{0,4},{4,0},{8,12},{12,8},{16,20},{20,16},{24,28},{28,24},{32,36},... | collective-permute-start | bytes 2654216 | tf_op jit(solution)/shard_map/ppermute | solution.py:27
  (87 shorter events, 38.7 us)
Async XLA Ops:
  24.2 14.5 %copy-start.9 = (s32[1,1,27,2,3]{2,3,4,1,0:T(2,128)S(1)}, s32[1,1,27,2,3]{2,3,4,1,0:T(2,128)}, u32[]{:S(2)}) copy-start(s32[1,1,27,2,3]{2,3,4,1,0:T(2,128)} %param.10) | copy-start | bytes 1948
  24.2 14.7 %copy-start.10 = (s32[1,1,27]{2,1,0:T(1,128)S(1)}, s32[1,1,27]{2,1,0:T(1,128)}, u32[]{:S(2)}) copy-start(s32[1,1,27]{2,1,0:T(1,128)} %param.11) | copy-start | bytes 328
  24.2 15.1 %copy-start.7 = (bf16[1,1,8,128,256]{4,3,2,1,0:T(8,128)(2,1)S(1)}, bf16[1,1,8,128,256]{4,3,2,1,0:T(8,128)(2,1)}, u32[]{:S(2)}) copy-start(bf16[1,1,8,128,256]{4,3,2,1,0:T(8,128)(2,1)} %param.7) | copy-start | bytes 1572868
  24.2 195.8 %all-to-all-start = ((bf16[64,2,128,256]{3,2,1,0:T(8,128)(2,1)}), bf16[64,2,128,256]{3,2,1,0:T(8,128)(2,1)}, u32[]{:S(2)}, u32[]{:S(2)}) async-start(bf16[64,2,128,256]{3,2,1,0:T(8,128)(2,1)} %bitcast.91), calls=%async_computation | async-start | bytes 16777216 | tf_op jit(solution)/shard_map/all_to_all | solution.py:46
  37.7 214.5 %all-gather.2.cloned.1.call-start = ((), (), s32[]{:S(2)}) async-start(), calls=%async_computation.4 | async-start | bytes 4423680 | tf_op jit(solution)/shard_map/all_gather | solution.py:48
  38.5 287.5 %reduce-scatter.2.cloned.1.call-start = ((), (), s32[]{:S(2)}) async-start(), calls=%async_computation.3 | async-start | bytes 8847360 | tf_op jit(solution)/shard_map/reduce_scatter | solution.py:97
  242.8 3.6 slice-start
  242.8 4.4 slice-start.1
  243.5 2.7 copy-start
  252.2 28.8 %copy-start.8 = (pred[136,81]{1,0:T(8,128)(4,1)}, pred[136,81]{1,0:T(8,128)(4,1)S(1)}, u32[]{:S(2)}) copy-start(pred[136,81]{1,0:T(8,128)(4,1)S(1)} %iota_compare_fusion.1) | copy-start | bytes 33052
  302.4 192.3 %all-to-all-start.1 = ((bf16[64,2,128,256]{3,2,1,0:T(8,128)(2,1)}), bf16[64,2,128,256]{3,2,1,0:T(8,128)(2,1)}, u32[]{:S(2)}, u32[]{:S(2)}) async-start(bf16[64,2,128,256]{3,2,1,0:T(8,128)(2,1)} %bitcast.90), calls=%async_computation.2 | async-start | bytes 16777216 | tf_op jit(solution)/shard_map/all_to_all | solution.py:73
  328.4 1.2 copy-start.2
  330.5 12.4 %copy-start.1 = (bf16[27,256,256]{2,1,0:T(8,128)(2,1)S(1)}, bf16[27,256,256]{2,1,0:T(8,128)(2,1)}, u32[]{:S(2)}) copy-start(bf16[27,256,256]{2,1,0:T(8,128)(2,1)} %all-gather.2.cloned.1.call-done) | copy-start | bytes 10616836
  330.5 8.8 %collective-permute-start = (f32[221184]{0:T(1024)}, f32[221184]{0:T(1024)}, u32[]{:S(2)}, u32[]{:S(2)}) collective-permute-start(f32[221184]{0:T(1024)} %dynamic_slice.37), channel_id=1, source_target_pairs={{0,4},{4,0},{8,12},{12,8},{16,20},{20,16},{24,28},{28,24},{32,36},... | collective-permute-start | bytes 2654216 | tf_op jit(solution)/shard_map/ppermute | solution.py:19
  331.5 7.9 %copy-start.3 = (f32[216,2,8,128]{3,1,2,0:T(2,128)S(1)}, f32[216,2,8,128]{3,1,2,0:T(2,128)}, u32[]{:S(2)}) copy-start(f32[216,2,8,128]{3,1,2,0:T(2,128)} %copy-done.2) | copy-start | bytes 5308420
  340.7 1.1 copy-start.5
  341.7 20.5 %collective-permute-start.1 = (f32[110592]{0:T(1024)}, f32[110592]{0:T(1024)}, u32[]{:S(2)}, u32[]{:S(2)}) collective-permute-start(f32[110592]{0:T(1024)} %dynamic_slice.39), channel_id=1, source_target_pairs={{0,8},{4,12},{8,0},{12,4},{16,24},{20,28},{24,16},{28,20},{32,40},... | collective-permute-start | bytes 1327112 | tf_op jit(solution)/shard_map/ppermute | solution.py:19
  347.0 15.3 %copy-start.6 = (f32[221184]{0:T(1024)S(1)}, f32[221184]{0:T(1024)}, u32[]{:S(2)}) copy-start(f32[221184]{0:T(1024)} %copy-done.5) | copy-start | bytes 2654212
  363.3 15.2 %collective-permute-start.2 = (f32[55296]{0:T(1024)S(1)}, f32[55296]{0:T(1024)S(1)}, u32[]{:S(2)}, u32[]{:S(2)}) collective-permute-start(f32[55296]{0:T(1024)S(1)} %dynamic_slice.41), channel_id=1, source_target_pairs={{0,16},{4,20},{8,24},{12,28},{16,0},{20,4},{24,8},{28,12},{32,48},... | collective-permute-start | bytes 663560 | tf_op jit(solution)/shard_map/ppermute | solution.py:19
  494.7 7.0 %collective-permute-start.3 = (f32[27648]{0:T(1024)S(1)}, f32[27648]{0:T(1024)S(1)}, u32[]{:S(2)}, u32[]{:S(2)}) collective-permute-start(f32[27648]{0:T(1024)S(1)} %dynamic_slice.43), channel_id=1, source_target_pairs={{0,32},{4,36},{8,40},{12,44},{16,48},{20,52},{24,56},{28,60},{32,0... | collective-permute-start | bytes 331784 | tf_op jit(solution)/shard_map/ppermute | solution.py:19
  501.8 4.0 collective-permute-start.4
  506.0 7.2 %collective-permute-start.5 = (f32[6912]{0:T(1024)S(1)}, f32[6912]{0:T(1024)S(1)}, u32[]{:S(2)}, u32[]{:S(2)}) collective-permute-start(f32[6912]{0:T(1024)S(1)} %dynamic_slice.47), channel_id=1, source_target_pairs={{0,128},{4,132},{8,136},{12,140},{16,144},{20,148},{24,152},{28,15... | collective-permute-start | bytes 82952 | tf_op jit(solution)/shard_map/ppermute | solution.py:19
  513.3 6.7 %collective-permute-start.6 = (f32[6912]{0:T(1024)S(1)}, f32[6912]{0:T(1024)S(1)}, u32[]{:S(2)}, u32[]{:S(2)}) collective-permute-start(f32[6912]{0:T(1024)S(1)} %dynamic-slice_add_fusion.5), channel_id=1, source_target_pairs={{0,128},{4,132},{8,136},{12,140},{16,144},{20,148},{24,152},{28,15... | collective-permute-start | bytes 82952 | tf_op jit(solution)/shard_map/ppermute | solution.py:27
  520.0 4.3 collective-permute-start.7
  524.3 4.0 collective-permute-start.8
  528.4 15.4 %collective-permute-start.9 = (f32[55296]{0:T(1024)S(1)}, f32[55296]{0:T(1024)S(1)}, u32[]{:S(2)}, u32[]{:S(2)}) collective-permute-start(f32[55296]{0:T(1024)S(1)} %maximum_select_fusion.3), channel_id=1, source_target_pairs={{0,16},{4,20},{8,24},{12,28},{16,0},{20,4},{24,8},{28,12},{32,48},... | collective-permute-start | bytes 663560 | tf_op jit(solution)/shard_map/ppermute | solution.py:27
  543.8 16.1 %copy-start.4 = (f32[8,32768]{1,0:T(8,128)S(1)}, f32[8,32768]{1,0:T(8,128)}, u32[]{:S(2)}) copy-start(f32[8,32768]{1,0:T(8,128)} %fusion.23) | copy-start | bytes 3145732
  543.8 7.2 %collective-permute-start.10 = (f32[110592]{0:T(1024)S(1)}, f32[110592]{0:T(1024)S(1)}, u32[]{:S(2)}, u32[]{:S(2)}) collective-permute-start(f32[110592]{0:T(1024)S(1)} %maximum_select_fusion.2), channel_id=1, source_target_pairs={{0,8},{4,12},{8,0},{12,4},{16,24},{20,28},{24,16},{28,20},{32,40},... | collective-permute-start | bytes 1327112 | tf_op jit(solution)/shard_map/ppermute | solution.py:27
  551.2 10.8 %collective-permute-start.11 = (f32[221184]{0:T(1024)S(1)}, f32[221184]{0:T(1024)S(1)}, u32[]{:S(2)}, u32[]{:S(2)}) collective-permute-start(f32[221184]{0:T(1024)S(1)} %maximum_select_fusion.1), channel_id=1, source_target_pairs={{0,4},{4,0},{8,12},{12,8},{16,20},{20,16},{24,28},{28,24},{32,36},... | collective-permute-start | bytes 2654216 | tf_op jit(solution)/shard_map/ppermute | solution.py:27
Sparse Core Ops, SparseCore 0:
  40.3 46.0 all-gather.1
  252.3 73.5 reduce-scatter.1

commit v6 on v5

--- a/solution.py
+++ b/solution.py
@@ -6,6 +6,27 @@
 
 def _onehot(index, size, dtype):
     return (index[..., None] == jnp.arange(size, dtype=index.dtype)).astype(dtype)
+
+
+def _direct_sum(buf, axis, low, width):
+    size = lax.axis_size(axis)
+    group = 1 << width
+    me = lax.axis_index(axis)
+    mine = (me >> low) & (group - 1)
+    part = buf.shape[0] // group
+    chunks = buf.reshape(group, part)
+    total = lax.dynamic_index_in_dim(chunks, mine, 0, keepdims=False)
+    for j in range(1, group):
+        pairs = [(i, i ^ (j << low)) for i in range(size)]
+        send = lax.dynamic_index_in_dim(chunks, mine ^ j, 0, keepdims=False)
+        total = total + lax.ppermute(send, axis, pairs)
+    gathered = [total]
+    for j in range(1, group):
+        pairs = [(i, i ^ (j << low)) for i in range(size)]
+        gathered.append(lax.ppermute(total, axis, pairs))
+    stacked = jnp.stack(gathered)
+    order = jnp.arange(group, dtype=mine.dtype) ^ mine
+    return jnp.take(stacked, order, axis=0).reshape(-1)
 
 
 def _halve(buf, axis, k):
@@ -103,9 +124,9 @@
     for k in range(early):
         buf = _halve(buf, "dp", k)
     buf, returned, produced, own_grad = lax.optimization_barrier((buf, returned, produced, own_grad))
-    for k in range(early, steps):
-        buf = _halve(buf, "dp", k)
-    for k in reversed(range(steps)):
+    if steps > early:
+        buf = _direct_sum(buf, "dp", early, steps - early)
+    for k in reversed(range(early)):
         buf = _double(buf, "dp", k)
     kernel_grad = buf.reshape(scattered.shape) / divisor
 

time: 576 us -> 576 us (level)
  waiting for transfers between devices: 337 us -> 319 us
  starting transfers between devices: 47.3 us -> 64.1 us
    ppermute x0 -> x14, starting transfers between devices: none -> 27 us  [the longest x7 15.3 us: _direct_sum(): total = total + lax.ppermute(send, axis, pairs)]
    ppermute x6 -> x3, waiting for transfers between devices: 14.6 us -> 2.54 us  [_double(): other = lax.ppermute(buf, axis, pairs)]
    ppermute x6 -> x3, waiting for transfers between devices: 24.1 us -> 12.2 us  [_halve(): return keep + lax.ppermute(send, axis, pairs)]
    ppermute x6 -> x3, starting transfers between devices: 8.7 us -> 2.41 us  [_halve(): return keep + lax.ppermute(send, axis, pairs)]
    ppermute x0 -> x14, waiting for transfers between devices: none -> 5.85 us  [the longest x7 3.32 us: _direct_sum(): gathered.append(lax.ppermute(total, axis, pairs))]
    ppermute x6 -> x3, starting transfers between devices: 14.9 us -> 10.8 us  [_double(): other = lax.ppermute(buf, axis, pairs)]
  transfers between devices with their start and end apart: 16 -> 24, of which waited for: 13 -> 11; matrix products, arithmetic and copies ran while one was open for 26% -> 26% of each run, Pallas kernels for 0% -> 0%
where the time goes in v6:
time: 576 us; the launch traced here: 571 us
  waiting for transfers between devices  319 us (55%)
  local copies, waits for them, and re-layouts  95.9 us (17%)
  matrix products  73.9 us (13%)
  starting transfers between devices  64.1 us (11%)
  between operations  14.7 us (3%)
    all_to_all x1, waiting for transfers between devices, _section(): lax.all_to_all(outgoing, 'dp', split_axis=0, concat_axis=0, tiled=True)  168 us
    all_to_all x1, waiting for transfers between devices, _section(): lax.all_to_all(ghost_grad.reshape(peer_total, slot_cap, brick_rows, chann...  116 us
    unnamed x42, local copies, waits for them, and re-layouts  85.1 us
    ppermute x7, starting transfers between devices, _direct_sum(): total = total + lax.ppermute(send, axis, pairs)  15.3 us
    reduce_scatter x1, waiting for transfers between devices, _section(): lax.psum_scatter(partial_value, 'fsdp', scatter_dimension=1, tiled=True)  13.5 us
    all_to_all x1, starting transfers between devices, _section(): lax.all_to_all(outgoing, 'dp', split_axis=0, concat_axis=0, tiled=True)  13.5 us
    dot_general x1, matrix products, _section(): jnp.dot(out_pick, contrib.reshape(pair_total, brick_rows * channels), pre...  13.2 us
    dot_general x1, matrix products, _section(): jnp.dot(src_pick[brick_total:], backward, precision=lax.Precision.HIGHEST...  12.2 us
  transfers between devices with their start and end apart: 24, of which 11 were waited for; matrix products, arithmetic and copies ran while one was open for 26% of the time, Pallas kernels for 0%

profile of v6, /device:TPU:1, one launch (start us, length us, event | category | flops | bytes accessed | tf_op | source)
XLA Modules:
  0.0 570.7 jit_solution(7613270470632967455)
XLA Ops:
  9.4 5.6 convolution_convert_fusion.1
  15.0 9.2 %copy.26 = bf16[16,8,128,256]{3,2,1,0:T(8,128)(2,1)} copy(bf16[16,8,128,256]{3,1,2,0:T(8,128)(2,1)} %bitcast.95) | data formatting | bytes 16777216
  24.2 13.5 %all-to-all-start = ((bf16[64,2,128,256]{3,2,1,0:T(8,128)(2,1)}), bf16[64,2,128,256]{3,2,1,0:T(8,128)(2,1)}, u32[]{:S(2)}, u32[]{:S(2)}) async-start(bf16[64,2,128,256]{3,2,1,0:T(8,128)(2,1)} %bitcast.93), calls=%async_computation | async-start | bytes 16777216 | tf_op jit(solution)/shard_map/all_to_all | solution.py:67
  43.1 2.8 slice.31
  46.0 5.8 %fusion.17 = f32[81,32768]{1,0:T(8,128)} fusion(bf16[8,32768]{1,0:T(8,128)(2,1)S(1)} %bitcast.104, bf16[81,136]{1,0:T(8,128)(2,1)S(1)} %fusion.11), kind=kOutput, calls=%fused_computation.42 | convolution fusion | flops 42467328 | bytes 11163648 | tf_op jit(solution)/shard_map/dot_general | solution.py:102
  51.8 168.2 %all-to-all-done = bf16[64,2,128,256]{3,2,1,0:T(8,128)(2,1)} async-done(((bf16[64,2,128,256]{3,2,1,0:T(8,128)(2,1)}), bf16[64,2,128,256]{3,2,1,0:T(8,128)(2,1)}, u32[]{:S(2)}, u32[]{:S(2)}) %all-to-all-start) | async-done | bytes 8388640 | tf_op jit(solution)/shard_map/all_to_all | solution.py:67
  220.0 12.5 %copy.27 = bf16[16,8,128,256]{3,1,2,0:T(8,128)(2,1)} copy(bf16[16,8,128,256]{3,2,1,0:T(8,128)(2,1)} %bitcast.20) | data formatting | bytes 16777216
  232.5 8.6 %fusion = bf16[81,32768]{1,0:T(8,128)(2,1)S(1)} fusion(f32[81,32768]{1,0:T(8,128)} %fusion.17, bf16[128,32768]{1,0:T(8,128)(2,1)} %bitcast.91, bf16[81,136]{1,0:T(8,128)(2,1)S(1)} %fusion.11), kind=kOutput, calls=%fused_computation.4 | convolution fusion | flops 684785664 | bytes 24336384 | tf_op jit(solution)/shard_map/dot_general | solution.py:103
  243.2 2.7 copy-done
  247.0 5.0 convolution_bitcast_fusion
  252.0 5.2 fusion.5
  257.2 5.9 %pad.13 = f32[88,128,256]{2,1,0:T(8,128)} pad(f32[81,128,256]{2,1,0:T(8,128)S(1)} %bitcast.90, f32[]{:T(128)} %constant.90), padding=0_7x0_0x0_0 | pad | bytes 22151172
  263.1 17.7 %copy.32 = f32[11,8,128,256]{3,1,2,0:T(8,128)} copy(f32[11,8,128,256]{3,2,1,0:T(8,128)} %bitcast.89) | data formatting | bytes 23068672
  280.8 12.2 %convolution_convert_fusion = bf16[128,32768]{1,0:T(8,128)(2,1)} fusion(f32[81,32768]{1,0:T(8,128)} %bitcast.80, pred[136,81]{1,0:T(8,128)(4,1)S(1)} %iota_compare_fusion.1), kind=kOutput, calls=%fused_computation.1 | convolution fusion | flops 4081057792 | bytes 19021824 | tf_op jit(solution)/shard_map/dot_general | solution.py:86
  293.1 9.2 %copy.33 = bf16[16,8,128,256]{3,2,1,0:T(8,128)(2,1)} copy(bf16[16,8,128,256]{3,1,2,0:T(8,128)(2,1)} %bitcast.96) | data formatting | bytes 16777216
  302.2 10.0 %all-to-all-start.1 = ((bf16[64,2,128,256]{3,2,1,0:T(8,128)(2,1)}), bf16[64,2,128,256]{3,2,1,0:T(8,128)(2,1)}, u32[]{:S(2)}, u32[]{:S(2)}) async-start(bf16[64,2,128,256]{3,2,1,0:T(8,128)(2,1)} %bitcast.92), calls=%async_computation.2 | async-start | bytes 16777216 | tf_op jit(solution)/shard_map/all_to_all | solution.py:94
  312.2 13.5 %reduce-scatter.2.cloned.1.call-done = f32[27,64,256]{2,1,0:T(8,128)} async-done(((f32[27,256,256]{2,1,0:T(8,128)}), f32[27,64,256]{2,1,0:T(8,128)}) %reduce-scatter.2.cloned.1.call-update) | async-done | bytes 1769488 | tf_op jit(solution)/shard_map/reduce_scatter | solution.py:118
  331.4 7.9 %fusion.23 = f32[8,32768]{1,0:T(8,128)} fusion(f32[81,32768]{1,0:T(8,128)} %bitcast.81, pred[136,81]{1,0:T(8,128)(4,1)} %copy-done.8), kind=kOutput, calls=%fused_computation.50 | convolution fusion | flops 254803968 | bytes 12583936 | tf_op jit(solution)/shard_map/dot_general | solution.py:90
  342.9 4.1 fusion.3
  346.9 4.8 slice_bitcast_fusion
  351.8 10.2 %collective-permute-done.1 = f32[110592]{0:T(1024)} collective-permute-done((f32[110592]{0:T(1024)}, f32[110592]{0:T(1024)}, u32[]{:S(2)}, u32[]{:S(2)}) %collective-permute-start.1) | collective-permute-done | bytes 442400 | tf_op jit(solution)/shard_map/ppermute | solution.py:40
  363.2 13.2 %fusion.8 = bf16[8,128,256]{2,0,1:T(8,128)(2,1)S(1)} fusion(f32[128,256,81]{1,0,2:T(8,128)} %slice_bitcast_fusion, s32[81]{0:T(128)S(1)} %eq.90), kind=kOutput, calls=%fused_computation.16 | convolution fusion | flops 255066752 | bytes 11141444 | tf_op jit(solution)/shard_map/dot_general | solution.py:108
  378.4 116.1 %all-to-all-done.1 = bf16[64,2,128,256]{3,2,1,0:T(8,128)(2,1)} async-done(((bf16[64,2,128,256]{3,2,1,0:T(8,128)(2,1)}), bf16[64,2,128,256]{3,2,1,0:T(8,128)(2,1)}, u32[]{:S(2)}, u32[]{:S(2)}) %all-to-all-start.1) | async-done | bytes 8388640 | tf_op jit(solution)/shard_map/all_to_all | solution.py:94
  495.1 4.9 collective-permute-start.3
  503.3 3.7 collective-permute-start.7
  507.0 3.4 collective-permute-start.9
  516.6 3.2 collective-permute-start.13
  520.8 3.5 collective-permute-start.15
  529.3 3.2 collective-permute-start.17
  532.5 12.4 %copy.36 = bf16[16,8,128,256]{3,1,2,0:T(8,128)(2,1)} copy(bf16[16,8,128,256]{3,2,1,0:T(8,128)(2,1)} %bitcast.53) | data formatting | bytes 16777216
  545.1 4.8 fusion.12
  552.3 7.5 %collective-permute-start.19 = (f32[221184]{0:T(1024)S(1)}, f32[221184]{0:T(1024)S(1)}, u32[]{:S(2)}, u32[]{:S(2)}) collective-permute-start(f32[221184]{0:T(1024)S(1)} %maximum_select_fusion.1), channel_id=1, source_target_pairs={{0,4},{4,0},{8,12},{12,8},{16,20},{20,16},{24,28},{28,24},{32,36},... | collective-permute-start | bytes 2654216 | tf_op jit(solution)/shard_map/ppermute | solution.py:48
  (112 shorter events, 45.9 us)
Async XLA Ops:
  24.2 14.7 %copy-start.9 = (s32[1,1,27,2,3]{2,3,4,1,0:T(2,128)S(1)}, s32[1,1,27,2,3]{2,3,4,1,0:T(2,128)}, u32[]{:S(2)}) copy-start(s32[1,1,27,2,3]{2,3,4,1,0:T(2,128)} %param.10) | copy-start | bytes 1948
  24.2 15.0 %copy-start.10 = (s32[1,1,27]{2,1,0:T(1,128)S(1)}, s32[1,1,27]{2,1,0:T(1,128)}, u32[]{:S(2)}) copy-start(s32[1,1,27]{2,1,0:T(1,128)} %param.11) | copy-start | bytes 328
  24.2 15.3 %copy-start.7 = (bf16[1,1,8,128,256]{4,3,2,1,0:T(8,128)(2,1)S(1)}, bf16[1,1,8,128,256]{4,3,2,1,0:T(8,128)(2,1)}, u32[]{:S(2)}) copy-start(bf16[1,1,8,128,256]{4,3,2,1,0:T(8,128)(2,1)} %param.7) | copy-start | bytes 1572868
  24.2 195.8 %all-to-all-start = ((bf16[64,2,128,256]{3,2,1,0:T(8,128)(2,1)}), bf16[64,2,128,256]{3,2,1,0:T(8,128)(2,1)}, u32[]{:S(2)}, u32[]{:S(2)}) async-start(bf16[64,2,128,256]{3,2,1,0:T(8,128)(2,1)} %bitcast.93), calls=%async_computation | async-start | bytes 16777216 | tf_op jit(solution)/shard_map/all_to_all | solution.py:67
  37.7 214.3 %all-gather.2.cloned.1.call-start = ((), (), s32[]{:S(2)}) async-start(), calls=%async_computation.4 | async-start | bytes 4423680 | tf_op jit(solution)/shard_map/all_gather | solution.py:69
  38.4 287.2 %reduce-scatter.2.cloned.1.call-start = ((), (), s32[]{:S(2)}) async-start(), calls=%async_computation.3 | async-start | bytes 8847360 | tf_op jit(solution)/shard_map/reduce_scatter | solution.py:118
  252.0 28.8 %copy-start.8 = (pred[136,81]{1,0:T(8,128)(4,1)}, pred[136,81]{1,0:T(8,128)(4,1)S(1)}, u32[]{:S(2)}) copy-start(pred[136,81]{1,0:T(8,128)(4,1)S(1)} %iota_compare_fusion.1) | copy-start | bytes 33052
  302.2 192.3 %all-to-all-start.1 = ((bf16[64,2,128,256]{3,2,1,0:T(8,128)(2,1)}), bf16[64,2,128,256]{3,2,1,0:T(8,128)(2,1)}, u32[]{:S(2)}, u32[]{:S(2)}) async-start(bf16[64,2,128,256]{3,2,1,0:T(8,128)(2,1)} %bitcast.92), calls=%async_computation.2 | async-start | bytes 16777216 | tf_op jit(solution)/shard_map/all_to_all | solution.py:94
  330.3 12.6 %copy-start.1 = (bf16[27,256,256]{2,1,0:T(8,128)(2,1)S(1)}, bf16[27,256,256]{2,1,0:T(8,128)(2,1)}, u32[]{:S(2)}) copy-start(bf16[27,256,256]{2,1,0:T(8,128)(2,1)} %all-gather.2.cloned.1.call-done) | copy-start | bytes 10616836
  330.3 9.0 %collective-permute-start = (f32[221184]{0:T(1024)}, f32[221184]{0:T(1024)}, u32[]{:S(2)}, u32[]{:S(2)}) collective-permute-start(f32[221184]{0:T(1024)} %dynamic_slice.44), channel_id=1, source_target_pairs={{0,4},{4,0},{8,12},{12,8},{16,20},{20,16},{24,28},{28,24},{32,36},... | collective-permute-start | bytes 2654216 | tf_op jit(solution)/shard_map/ppermute | solution.py:40
  331.4 7.9 %copy-start.3 = (f32[216,2,8,128]{3,1,2,0:T(2,128)S(1)}, f32[216,2,8,128]{3,1,2,0:T(2,128)}, u32[]{:S(2)}) copy-start(f32[216,2,8,128]{3,1,2,0:T(2,128)} %copy-done.2) | copy-start | bytes 5308420
  341.7 20.3 %collective-permute-start.1 = (f32[110592]{0:T(1024)}, f32[110592]{0:T(1024)}, u32[]{:S(2)}, u32[]{:S(2)}) collective-permute-start(f32[110592]{0:T(1024)} %dynamic_slice.46), channel_id=1, source_target_pairs={{0,8},{4,12},{8,0},{12,4},{16,24},{20,28},{24,16},{28,20},{32,40},... | collective-permute-start | bytes 1327112 | tf_op jit(solution)/shard_map/ppermute | solution.py:40
  346.9 15.1 %copy-start.6 = (f32[221184]{0:T(1024)S(1)}, f32[221184]{0:T(1024)}, u32[]{:S(2)}) copy-start(f32[221184]{0:T(1024)} %copy-done.5) | copy-start | bytes 2654212
  363.1 15.2 %collective-permute-start.2 = (f32[55296]{0:T(1024)S(1)}, f32[55296]{0:T(1024)S(1)}, u32[]{:S(2)}, u32[]{:S(2)}) collective-permute-start(f32[55296]{0:T(1024)S(1)} %dynamic_slice.48), channel_id=1, source_target_pairs={{0,16},{4,20},{8,24},{12,28},{16,0},{20,4},{24,8},{28,12},{32,48},... | collective-permute-start | bytes 663560 | tf_op jit(solution)/shard_map/ppermute | solution.py:40
  495.1 11.9 %collective-permute-start.3 = (f32[6912]{0:T(1024)S(1)}, f32[6912]{0:T(1024)S(1)}, u32[]{:S(2)}, u32[]{:S(2)}) collective-permute-start(f32[6912]{0:T(1024)S(1)} %get-tuple-element.17), channel_id=1, source_target_pairs={{0,32},{4,36},{8,40},{12,44},{16,48},{20,52},{24,56},{28,60},{32,0... | collective-permute-start | bytes 82952 | tf_op jit(solution)/shard_map/ppermute | solution.py:22
  500.0 7.0 %collective-permute-start.4 = (f32[6912]{0:T(1024)S(1)}, f32[6912]{0:T(1024)S(1)}, u32[]{:S(2)}, u32[]{:S(2)}) collective-permute-start(f32[6912]{0:T(1024)S(1)} %get-tuple-element.23), channel_id=1, source_target_pairs={{0,64},{4,68},{8,72},{12,76},{16,80},{20,84},{24,88},{28,92},{32,9... | collective-permute-start | bytes 82952 | tf_op jit(solution)/shard_map/ppermute | solution.py:22
  500.0 10.4 %collective-permute-start.5 = (f32[6912]{0:T(1024)S(1)}, f32[6912]{0:T(1024)S(1)}, u32[]{:S(2)}, u32[]{:S(2)}) collective-permute-start(f32[6912]{0:T(1024)S(1)} %get-tuple-element.22), channel_id=1, source_target_pairs={{0,96},{4,100},{8,104},{12,108},{16,112},{20,116},{24,120},{28,124... | collective-permute-start | bytes 82952 | tf_op jit(solution)/shard_map/ppermute | solution.py:22
  502.3 8.1 %collective-permute-start.6 = (f32[6912]{0:T(1024)S(1)}, f32[6912]{0:T(1024)S(1)}, u32[]{:S(2)}, u32[]{:S(2)}) collective-permute-start(f32[6912]{0:T(1024)S(1)} %get-tuple-element.21), channel_id=1, source_target_pairs={{0,128},{4,132},{8,136},{12,140},{16,144},{20,148},{24,152},{28,15... | collective-permute-start | bytes 82952 | tf_op jit(solution)/shard_map/ppermute | solution.py:22
  503.3 7.1 %collective-permute-start.7 = (f32[6912]{0:T(1024)S(1)}, f32[6912]{0:T(1024)S(1)}, u32[]{:S(2)}, u32[]{:S(2)}) collective-permute-start(f32[6912]{0:T(1024)S(1)} %get-tuple-element.20), channel_id=1, source_target_pairs={{0,160},{4,164},{8,168},{12,172},{16,176},{20,180},{24,184},{28,18... | collective-permute-start | bytes 82952 | tf_op jit(solution)/shard_map/ppermute | solution.py:22
  507.0 5.3 collective-permute-start.8
  507.0 5.9 %collective-permute-start.9 = (f32[6912]{0:T(1024)S(1)}, f32[6912]{0:T(1024)S(1)}, u32[]{:S(2)}, u32[]{:S(2)}) collective-permute-start(f32[6912]{0:T(1024)S(1)} %get-tuple-element.18), channel_id=1, source_target_pairs={{0,224},{4,228},{8,232},{12,236},{16,240},{20,244},{24,248},{28,25... | collective-permute-start | bytes 82952 | tf_op jit(solution)/shard_map/ppermute | solution.py:22
  513.0 7.8 %collective-permute-start.10 = (f32[6912]{0:T(1024)S(1)}, f32[6912]{0:T(1024)S(1)}, u32[]{:S(2)}, u32[]{:S(2)}) collective-permute-start(f32[6912]{0:T(1024)S(1)} %add_add_fusion), channel_id=1, source_target_pairs={{0,32},{4,36},{8,40},{12,44},{16,48},{20,52},{24,56},{28,60},{32,0... | collective-permute-start | bytes 82952 | tf_op jit(solution)/shard_map/ppermute | solution.py:26
  513.9 10.3 %collective-permute-start.11 = (f32[6912]{0:T(1024)S(1)}, f32[6912]{0:T(1024)S(1)}, u32[]{:S(2)}, u32[]{:S(2)}) collective-permute-start(f32[6912]{0:T(1024)S(1)} %add_add_fusion), channel_id=1, source_target_pairs={{0,64},{4,68},{8,72},{12,76},{16,80},{20,84},{24,88},{28,92},{32,9... | collective-permute-start | bytes 82952 | tf_op jit(solution)/shard_map/ppermute | solution.py:26
  514.2 10.6 %collective-permute-start.12 = (f32[6912]{0:T(1024)S(1)}, f32[6912]{0:T(1024)S(1)}, u32[]{:S(2)}, u32[]{:S(2)}) collective-permute-start(f32[6912]{0:T(1024)S(1)} %add_add_fusion), channel_id=1, source_target_pairs={{0,96},{4,100},{8,104},{12,108},{16,112},{20,116},{24,120},{28,124... | collective-permute-start | bytes 82952 | tf_op jit(solution)/shard_map/ppermute | solution.py:26
  516.6 8.2 %collective-permute-start.13 = (f32[6912]{0:T(1024)S(1)}, f32[6912]{0:T(1024)S(1)}, u32[]{:S(2)}, u32[]{:S(2)}) collective-permute-start(f32[6912]{0:T(1024)S(1)} %add_add_fusion), channel_id=1, source_target_pairs={{0,128},{4,132},{8,136},{12,140},{16,144},{20,148},{24,152},{28,15... | collective-permute-start | bytes 82952 | tf_op jit(solution)/shard_map/ppermute | solution.py:26
  519.8 6.6 %collective-permute-start.14 = (f32[6912]{0:T(1024)S(1)}, f32[6912]{0:T(1024)S(1)}, u32[]{:S(2)}, u32[]{:S(2)}) collective-permute-start(f32[6912]{0:T(1024)S(1)} %add_add_fusion), channel_id=1, source_target_pairs={{0,160},{4,164},{8,168},{12,172},{16,176},{20,180},{24,184},{28,18... | collective-permute-start | bytes 82952 | tf_op jit(solution)/shard_map/ppermute | solution.py:26
  520.8 5.7 collective-permute-start.15
  524.3 3.9 collective-permute-start.16
  529.3 15.6 %collective-permute-start.17 = (f32[55296]{0:T(1024)S(1)}, f32[55296]{0:T(1024)S(1)}, u32[]{:S(2)}, u32[]{:S(2)}) collective-permute-start(f32[55296]{0:T(1024)S(1)} %select_n.113), channel_id=1, source_target_pairs={{0,16},{4,20},{8,24},{12,28},{16,0},{20,4},{24,8},{28,12},{32,48},... | collective-permute-start | bytes 663560 | tf_op jit(solution)/shard_map/ppermute | solution.py:48
  544.9 14.8 %copy-start.4 = (f32[8,32768]{1,0:T(8,128)S(1)}, f32[8,32768]{1,0:T(8,128)}, u32[]{:S(2)}) copy-start(f32[8,32768]{1,0:T(8,128)} %fusion.23) | copy-start | bytes 3145732
  545.0 7.2 %collective-permute-start.18 = (f32[110592]{0:T(1024)S(1)}, f32[110592]{0:T(1024)S(1)}, u32[]{:S(2)}, u32[]{:S(2)}) collective-permute-start(f32[110592]{0:T(1024)S(1)} %maximum_select_fusion.2), channel_id=1, source_target_pairs={{0,8},{4,12},{8,0},{12,4},{16,24},{20,28},{24,16},{28,20},{32,40},... | collective-permute-start | bytes 1327112 | tf_op jit(solution)/shard_map/ppermute | solution.py:48
  552.3 9.5 %collective-permute-start.19 = (f32[221184]{0:T(1024)S(1)}, f32[221184]{0:T(1024)S(1)}, u32[]{:S(2)}, u32[]{:S(2)}) collective-permute-start(f32[221184]{0:T(1024)S(1)} %maximum_select_fusion.1), channel_id=1, source_target_pairs={{0,4},{4,0},{8,12},{12,8},{16,20},{20,16},{24,28},{28,24},{32,36},... | collective-permute-start | bytes 2654216 | tf_op jit(solution)/shard_map/ppermute | solution.py:48
  (5 other events, 13.0 us)
Sparse Core Ops, SparseCore 0:
  40.3 46.0 all-gather.1
  252.1 73.5 reduce-scatter.1

commit v7 on v5

--- a/solution.py
+++ b/solution.py
@@ -40,9 +40,10 @@
     own_flat = own_rows.reshape(brick_total, brick_rows * channels)
     up_flat = upstream_rows.reshape(brick_total, brick_rows * channels)
 
-    send_pick = _onehot(senders.reshape(-1), brick_total, jnp.bfloat16)
-    outgoing = jnp.dot(send_pick, own_flat, preferred_element_type=jnp.float32).astype(jnp.bfloat16)
-    outgoing = outgoing.reshape(peer_total, slot_cap, brick_rows, channels)
+    filled = senders >= 0
+    outgoing = jnp.where(
+        filled[:, :, None, None], own_rows[jnp.maximum(senders, 0)], jnp.zeros((), own_rows.dtype)
+    )
     incoming = lax.all_to_all(outgoing, "dp", split_axis=0, concat_axis=0, tiled=True)
 
     weights = lax.all_gather(kernel, "fsdp", axis=1, tiled=True)
@@ -105,9 +106,10 @@
     buf, returned, produced, own_grad = lax.optimization_barrier((buf, returned, produced, own_grad))
     for k in range(early, steps):
         buf = _halve(buf, "dp", k)
+    buf = buf / divisor
     for k in reversed(range(steps)):
         buf = _double(buf, "dp", k)
-    kernel_grad = buf.reshape(scattered.shape) / divisor
+    kernel_grad = buf.reshape(scattered.shape)
 
     owner_pick = _onehot(senders.reshape(-1), brick_total, jnp.bfloat16).T
     back_sum = jnp.dot(

time: 576 us -> 575 us (level)
  other arithmetic: 3.14 us -> 11.9 us
    unnamed x42 -> x45, local copies, waits for them, and re-layouts: 85 us -> 74.1 us
    gather x0 -> x1, local copies, waits for them, and re-layouts: none -> 7.52 us  [_section(): own_rows[jnp.maximum(senders, 0)]]
    select_n x0 -> x1, other arithmetic: none -> 7.34 us  [_section(): jnp.where(filled[:, :, None, None], own_rows[jnp.maximum(senders, 0)], jn...]
where the time goes in v7:
time: 575 us; the launch traced here: 571 us
  waiting for transfers between devices  337 us (59%)
  local copies, waits for them, and re-layouts  91.2 us (16%)
  matrix products  68.5 us (12%)
  starting transfers between devices  47.3 us (8%)
  between operations  14.8 us (3%)
  other arithmetic  11.9 us (2%)
    all_to_all x1, waiting for transfers between devices, _section(): lax.all_to_all(outgoing, 'dp', split_axis=0, concat_axis=0, tiled=True)  168 us
    all_to_all x1, waiting for transfers between devices, _section(): lax.all_to_all(ghost_grad.reshape(peer_total, slot_cap, brick_rows, chann...  116 us
    unnamed x45, local copies, waits for them, and re-layouts  74.1 us
    ppermute x6, waiting for transfers between devices, _halve(): return keep + lax.ppermute(send, axis, pairs)  24.1 us
    ppermute x6, starting transfers between devices, _double(): other = lax.ppermute(buf, axis, pairs)  14.9 us
    ppermute x6, waiting for transfers between devices, _double(): other = lax.ppermute(buf, axis, pairs)  14.5 us
    reduce_scatter x1, waiting for transfers between devices, _section(): lax.psum_scatter(partial_value, 'fsdp', scatter_dimension=1, tiled=True)  13.6 us
    all_to_all x1, starting transfers between devices, _section(): lax.all_to_all(outgoing, 'dp', split_axis=0, concat_axis=0, tiled=True)  13.5 us
  transfers between devices with their start and end apart: 16, of which 13 were waited for; matrix products, arithmetic and copies ran while one was open for 26% of the time, Pallas kernels for 0%

profile of v7, /device:TPU:1, one launch (start us, length us, event | category | flops | bytes accessed | tf_op | source)
XLA Modules:
  0.0 570.8 jit_solution(7093215341601539666)
XLA Ops:
  8.9 7.5 %gather_fusion = bf16[128,128,256]{2,1,0:T(8,128)(2,1)} fusion(bf16[8,128,256]{2,1,0:T(8,128)(2,1)} %bitcast.80, s32[1024]{0:T(1024)S(1)} %pad_clamp_fusion), kind=kCustom, calls=%fused_computation | custom fusion | bytes 16777728 | tf_op jit(solution)/shard_map/gather | solution.py:45
  16.4 7.3 %broadcast_select_fusion = bf16[64,2,128,256]{3,2,1,0:T(8,128)(2,1)} fusion(bf16[64,2,128,256]{3,2,1,0:T(8,128)(2,1)} %bitcast.96, pred[64,2]{1,0:T(8,128)(4,1)S(1)} %copy.18), kind=kLoop, calls=%fused_computation.8 | loop fusion | flops 4194304 | bytes 16777344 | tf_op jit(solution)/shard_map/jit(_where)/select_n | solution.py:44
  23.8 13.5 %all-to-all-start = ((bf16[64,2,128,256]{3,2,1,0:T(8,128)(2,1)}), bf16[64,2,128,256]{3,2,1,0:T(8,128)(2,1)}, u32[]{:S(2)}, u32[]{:S(2)}) async-start(bf16[64,2,128,256]{3,2,1,0:T(8,128)(2,1)} %broadcast_select_fusion), calls=%async_computation | async-start | bytes 16777216 | tf_op jit(solution)/shard_map/all_to_all | solution.py:47
  42.7 2.8 slice.31
  45.6 5.8 %fusion.15 = f32[81,32768]{1,0:T(8,128)} fusion(bf16[8,32768]{1,0:T(8,128)(2,1)S(1)} %bitcast.105, bf16[81,136]{1,0:T(8,128)(2,1)S(1)} %fusion.10), kind=kOutput, calls=%fused_computation.36 | convolution fusion | flops 42467328 | bytes 11163648 | tf_op jit(solution)/shard_map/dot_general | solution.py:82
  51.4 168.2 %all-to-all-done = bf16[64,2,128,256]{3,2,1,0:T(8,128)(2,1)} async-done(((bf16[64,2,128,256]{3,2,1,0:T(8,128)(2,1)}), bf16[64,2,128,256]{3,2,1,0:T(8,128)(2,1)}, u32[]{:S(2)}, u32[]{:S(2)}) %all-to-all-start) | async-done | bytes 8388640 | tf_op jit(solution)/shard_map/all_to_all | solution.py:47
  219.5 12.4 %copy.30 = bf16[16,8,128,256]{3,1,2,0:T(8,128)(2,1)} copy(bf16[16,8,128,256]{3,2,1,0:T(8,128)(2,1)} %bitcast.19) | data formatting | bytes 16777216
  232.0 8.8 %fusion = bf16[81,32768]{1,0:T(8,128)(2,1)S(1)} fusion(f32[81,32768]{1,0:T(8,128)} %fusion.15, bf16[128,32768]{1,0:T(8,128)(2,1)} %bitcast.93, bf16[81,136]{1,0:T(8,128)(2,1)S(1)} %fusion.10), kind=kOutput, calls=%fused_computation.3 | convolution fusion | flops 684785664 | bytes 24336384 | tf_op jit(solution)/shard_map/dot_general | solution.py:83
  243.0 2.7 copy-done.1
  246.7 5.0 convolution_bitcast_fusion
  251.8 5.2 fusion.5
  257.0 5.9 %pad.25 = f32[88,128,256]{2,1,0:T(8,128)} pad(f32[81,128,256]{2,1,0:T(8,128)S(1)} %bitcast.92, f32[]{:T(128)} %constant.62), padding=0_7x0_0x0_0 | pad | bytes 22151172
  262.9 17.7 %copy.35 = f32[11,8,128,256]{3,1,2,0:T(8,128)} copy(f32[11,8,128,256]{3,2,1,0:T(8,128)} %bitcast.91) | data formatting | bytes 23068672
  280.5 12.2 %convolution_convert_fusion = bf16[128,32768]{1,0:T(8,128)(2,1)} fusion(f32[81,32768]{1,0:T(8,128)} %bitcast.82, pred[136,81]{1,0:T(8,128)(4,1)S(1)} %iota_compare_fusion.1), kind=kOutput, calls=%fused_computation.1 | convolution fusion | flops 4081057792 | bytes 19021824 | tf_op jit(solution)/shard_map/dot_general | solution.py:66
  292.7 9.2 %copy.36 = bf16[16,8,128,256]{3,2,1,0:T(8,128)(2,1)} copy(bf16[16,8,128,256]{3,1,2,0:T(8,128)(2,1)} %bitcast.97) | data formatting | bytes 16777216
  301.9 10.0 %all-to-all-start.1 = ((bf16[64,2,128,256]{3,2,1,0:T(8,128)(2,1)}), bf16[64,2,128,256]{3,2,1,0:T(8,128)(2,1)}, u32[]{:S(2)}, u32[]{:S(2)}) async-start(bf16[64,2,128,256]{3,2,1,0:T(8,128)(2,1)} %bitcast.94), calls=%async_computation.2 | async-start | bytes 16777216 | tf_op jit(solution)/shard_map/all_to_all | solution.py:74
  311.9 13.6 %reduce-scatter.2.cloned.1.call-done = f32[27,64,256]{2,1,0:T(8,128)} async-done(((f32[27,256,256]{2,1,0:T(8,128)}), f32[27,64,256]{2,1,0:T(8,128)}) %reduce-scatter.2.cloned.1.call-update) | async-done | bytes 1769488 | tf_op jit(solution)/shard_map/reduce_scatter | solution.py:98
  331.0 7.9 %fusion.21 = f32[8,32768]{1,0:T(8,128)} fusion(f32[81,32768]{1,0:T(8,128)} %bitcast.83, pred[136,81]{1,0:T(8,128)(4,1)} %copy-done.9), kind=kOutput, calls=%fused_computation.44 | convolution fusion | flops 254803968 | bytes 12583936 | tf_op jit(solution)/shard_map/dot_general | solution.py:70
  342.5 4.1 fusion.3
  346.5 4.8 slice_bitcast_fusion
  351.4 10.4 %collective-permute-done.1 = f32[110592]{0:T(1024)} collective-permute-done((f32[110592]{0:T(1024)}, f32[110592]{0:T(1024)}, u32[]{:S(2)}, u32[]{:S(2)}) %collective-permute-start.1) | collective-permute-done | bytes 442400 | tf_op jit(solution)/shard_map/ppermute | solution.py:19
  362.9 13.2 %fusion.7 = bf16[8,128,256]{2,0,1:T(8,128)(2,1)S(1)} fusion(f32[128,256,81]{1,0,2:T(8,128)} %slice_bitcast_fusion, s32[81]{0:T(128)S(1)} %eq.88), kind=kOutput, calls=%fused_computation.15 | convolution fusion | flops 255066752 | bytes 11141444 | tf_op jit(solution)/shard_map/dot_general | solution.py:88
  378.1 116.1 %all-to-all-done.1 = bf16[64,2,128,256]{3,2,1,0:T(8,128)(2,1)} async-done(((bf16[64,2,128,256]{3,2,1,0:T(8,128)(2,1)}), bf16[64,2,128,256]{3,2,1,0:T(8,128)(2,1)}, u32[]{:S(2)}, u32[]{:S(2)}) %all-to-all-start.1) | async-done | bytes 8388640 | tf_op jit(solution)/shard_map/all_to_all | solution.py:74
  494.2 4.9 collective-permute-start.3
  501.4 3.9 collective-permute-done.4
  507.0 5.6 collective-permute-done.5
  513.8 5.7 collective-permute-done.6
  519.6 4.2 collective-permute-done.7
  527.9 3.0 collective-permute-start.9
  531.1 12.4 %copy.39 = bf16[16,8,128,256]{3,1,2,0:T(8,128)(2,1)} copy(bf16[16,8,128,256]{3,2,1,0:T(8,128)(2,1)} %bitcast.53) | data formatting | bytes 16777216
  543.7 4.8 fusion.11
  550.9 8.7 %collective-permute-start.11 = (f32[221184]{0:T(1024)S(1)}, f32[221184]{0:T(1024)S(1)}, u32[]{:S(2)}, u32[]{:S(2)}) collective-permute-start(f32[221184]{0:T(1024)S(1)} %maximum_select_fusion.1), channel_id=1, source_target_pairs={{0,4},{4,0},{8,12},{12,8},{16,20},{20,16},{24,28},{28,24},{32,36},... | collective-permute-start | bytes 2654216 | tf_op jit(solution)/shard_map/ppermute | solution.py:27
  (97 shorter events, 38.8 us)
Async XLA Ops:
  23.8 14.5 %copy-start.11 = (s32[1,1,27,2,3]{2,3,4,1,0:T(2,128)S(1)}, s32[1,1,27,2,3]{2,3,4,1,0:T(2,128)}, u32[]{:S(2)}) copy-start(s32[1,1,27,2,3]{2,3,4,1,0:T(2,128)} %param.10) | copy-start | bytes 1948
  23.8 14.7 %copy-start.12 = (s32[1,1,27]{2,1,0:T(1,128)S(1)}, s32[1,1,27]{2,1,0:T(1,128)}, u32[]{:S(2)}) copy-start(s32[1,1,27]{2,1,0:T(1,128)} %param.11) | copy-start | bytes 328
  23.8 14.9 %copy-start = (bf16[1,1,8,128,256]{4,3,2,1,0:T(8,128)(2,1)S(1)}, bf16[1,1,8,128,256]{4,3,2,1,0:T(8,128)(2,1)}, u32[]{:S(2)}) copy-start(bf16[1,1,8,128,256]{4,3,2,1,0:T(8,128)(2,1)} %param.6) | copy-start | bytes 1572868
  23.8 15.4 %copy-start.8 = (bf16[1,1,8,128,256]{4,3,2,1,0:T(8,128)(2,1)S(1)}, bf16[1,1,8,128,256]{4,3,2,1,0:T(8,128)(2,1)}, u32[]{:S(2)}) copy-start(bf16[1,1,8,128,256]{4,3,2,1,0:T(8,128)(2,1)} %param.7) | copy-start | bytes 1572868
  23.8 195.8 %all-to-all-start = ((bf16[64,2,128,256]{3,2,1,0:T(8,128)(2,1)}), bf16[64,2,128,256]{3,2,1,0:T(8,128)(2,1)}, u32[]{:S(2)}, u32[]{:S(2)}) async-start(bf16[64,2,128,256]{3,2,1,0:T(8,128)(2,1)} %broadcast_select_fusion), calls=%async_computation | async-start | bytes 16777216 | tf_op jit(solution)/shard_map/all_to_all | solution.py:47
  37.2 214.6 %all-gather.2.cloned.1.call-start = ((), (), s32[]{:S(2)}) async-start(), calls=%async_computation.4 | async-start | bytes 4423680 | tf_op jit(solution)/shard_map/all_gather | solution.py:49
  38.0 287.6 %reduce-scatter.2.cloned.1.call-start = ((), (), s32[]{:S(2)}) async-start(), calls=%async_computation.3 | async-start | bytes 8847360 | tf_op jit(solution)/shard_map/reduce_scatter | solution.py:98
  242.3 3.6 slice-start
  242.3 4.4 slice-start.1
  243.0 2.7 copy-start.1
  251.8 28.8 %copy-start.9 = (pred[136,81]{1,0:T(8,128)(4,1)}, pred[136,81]{1,0:T(8,128)(4,1)S(1)}, u32[]{:S(2)}) copy-start(pred[136,81]{1,0:T(8,128)(4,1)S(1)} %iota_compare_fusion.1) | copy-start | bytes 33052
  301.9 192.3 %all-to-all-start.1 = ((bf16[64,2,128,256]{3,2,1,0:T(8,128)(2,1)}), bf16[64,2,128,256]{3,2,1,0:T(8,128)(2,1)}, u32[]{:S(2)}, u32[]{:S(2)}) async-start(bf16[64,2,128,256]{3,2,1,0:T(8,128)(2,1)} %bitcast.94), calls=%async_computation.2 | async-start | bytes 16777216 | tf_op jit(solution)/shard_map/all_to_all | solution.py:74
  327.9 1.2 copy-start.3
  330.1 12.4 %copy-start.2 = (bf16[27,256,256]{2,1,0:T(8,128)(2,1)S(1)}, bf16[27,256,256]{2,1,0:T(8,128)(2,1)}, u32[]{:S(2)}) copy-start(bf16[27,256,256]{2,1,0:T(8,128)(2,1)} %all-gather.2.cloned.1.call-done) | copy-start | bytes 10616836
  330.1 8.8 %collective-permute-start = (f32[221184]{0:T(1024)}, f32[221184]{0:T(1024)}, u32[]{:S(2)}, u32[]{:S(2)}) collective-permute-start(f32[221184]{0:T(1024)} %dynamic_slice.37), channel_id=1, source_target_pairs={{0,4},{4,0},{8,12},{12,8},{16,20},{20,16},{24,28},{28,24},{32,36},... | collective-permute-start | bytes 2654216 | tf_op jit(solution)/shard_map/ppermute | solution.py:19
  331.0 7.9 %copy-start.4 = (f32[216,2,8,128]{3,1,2,0:T(2,128)S(1)}, f32[216,2,8,128]{3,1,2,0:T(2,128)}, u32[]{:S(2)}) copy-start(f32[216,2,8,128]{3,1,2,0:T(2,128)} %copy-done.3) | copy-start | bytes 5308420
  340.2 1.1 copy-start.6
  341.3 20.5 %collective-permute-start.1 = (f32[110592]{0:T(1024)}, f32[110592]{0:T(1024)}, u32[]{:S(2)}, u32[]{:S(2)}) collective-permute-start(f32[110592]{0:T(1024)} %dynamic_slice.39), channel_id=1, source_target_pairs={{0,8},{4,12},{8,0},{12,4},{16,24},{20,28},{24,16},{28,20},{32,40},... | collective-permute-start | bytes 1327112 | tf_op jit(solution)/shard_map/ppermute | solution.py:19
  346.5 15.2 %copy-start.7 = (f32[221184]{0:T(1024)S(1)}, f32[221184]{0:T(1024)}, u32[]{:S(2)}) copy-start(f32[221184]{0:T(1024)} %copy-done.6) | copy-start | bytes 2654212
  351.4 179.5 %copy-start.10 = (s32[1,1,64,2]{2,3,1,0:T(2,128)S(1)}, s32[1,1,64,2]{2,3,1,0:T(2,128)}, u32[]{:S(2)}) copy-start(s32[1,1,64,2]{2,3,1,0:T(2,128)} %param.9) | copy-start | bytes 1540
  362.8 15.3 %collective-permute-start.2 = (f32[55296]{0:T(1024)S(1)}, f32[55296]{0:T(1024)S(1)}, u32[]{:S(2)}, u32[]{:S(2)}) collective-permute-start(f32[55296]{0:T(1024)S(1)} %dynamic_slice.41), channel_id=1, source_target_pairs={{0,16},{4,20},{8,24},{12,28},{16,0},{20,4},{24,8},{28,12},{32,48},... | collective-permute-start | bytes 663560 | tf_op jit(solution)/shard_map/ppermute | solution.py:19
  494.2 7.0 %collective-permute-start.3 = (f32[27648]{0:T(1024)S(1)}, f32[27648]{0:T(1024)S(1)}, u32[]{:S(2)}, u32[]{:S(2)}) collective-permute-start(f32[27648]{0:T(1024)S(1)} %dynamic_slice.43), channel_id=1, source_target_pairs={{0,32},{4,36},{8,40},{12,44},{16,48},{20,52},{24,56},{28,60},{32,0... | collective-permute-start | bytes 331784 | tf_op jit(solution)/shard_map/ppermute | solution.py:19
  501.3 4.0 collective-permute-start.4
  505.5 7.2 %collective-permute-start.5 = (f32[6912]{0:T(1024)S(1)}, f32[6912]{0:T(1024)S(1)}, u32[]{:S(2)}, u32[]{:S(2)}) collective-permute-start(f32[6912]{0:T(1024)S(1)} %dynamic_slice.47), channel_id=1, source_target_pairs={{0,128},{4,132},{8,136},{12,140},{16,144},{20,148},{24,152},{28,15... | collective-permute-start | bytes 82952 | tf_op jit(solution)/shard_map/ppermute | solution.py:19
  512.8 6.7 %collective-permute-start.6 = (f32[6912]{0:T(1024)S(1)}, f32[6912]{0:T(1024)S(1)}, u32[]{:S(2)}, u32[]{:S(2)}) collective-permute-start(f32[6912]{0:T(1024)S(1)} %add_multiply_fusion), channel_id=1, source_target_pairs={{0,128},{4,132},{8,136},{12,140},{16,144},{20,148},{24,152},{28,15... | collective-permute-start | bytes 82952 | tf_op jit(solution)/shard_map/ppermute | solution.py:27
  519.5 4.3 collective-permute-start.7
  523.8 4.0 collective-permute-start.8
  527.9 15.7 %collective-permute-start.9 = (f32[55296]{0:T(1024)S(1)}, f32[55296]{0:T(1024)S(1)}, u32[]{:S(2)}, u32[]{:S(2)}) collective-permute-start(f32[55296]{0:T(1024)S(1)} %maximum_select_fusion.3), channel_id=1, source_target_pairs={{0,16},{4,20},{8,24},{12,28},{16,0},{20,4},{24,8},{28,12},{32,48},... | collective-permute-start | bytes 663560 | tf_op jit(solution)/shard_map/ppermute | solution.py:27
  543.5 16.1 %copy-start.5 = (f32[8,32768]{1,0:T(8,128)S(1)}, f32[8,32768]{1,0:T(8,128)}, u32[]{:S(2)}) copy-start(f32[8,32768]{1,0:T(8,128)} %fusion.21) | copy-start | bytes 3145732
  543.6 7.2 %collective-permute-start.10 = (f32[110592]{0:T(1024)S(1)}, f32[110592]{0:T(1024)S(1)}, u32[]{:S(2)}, u32[]{:S(2)}) collective-permute-start(f32[110592]{0:T(1024)S(1)} %maximum_select_fusion.2), channel_id=1, source_target_pairs={{0,8},{4,12},{8,0},{12,4},{16,24},{20,28},{24,16},{28,20},{32,40},... | collective-permute-start | bytes 1327112 | tf_op jit(solution)/shard_map/ppermute | solution.py:27
  550.9 10.8 %collective-permute-start.11 = (f32[221184]{0:T(1024)S(1)}, f32[221184]{0:T(1024)S(1)}, u32[]{:S(2)}, u32[]{:S(2)}) collective-permute-start(f32[221184]{0:T(1024)S(1)} %maximum_select_fusion.1), channel_id=1, source_target_pairs={{0,4},{4,0},{8,12},{12,8},{16,20},{20,16},{24,28},{28,24},{32,36},... | collective-permute-start | bytes 2654216 | tf_op jit(solution)/shard_map/ppermute | solution.py:27
Sparse Core Ops, SparseCore 0:
  39.9 46.0 all-gather.1
  251.9 73.6 reduce-scatter.1
